TPU v7x, 256 devices: a whole 4x4x8 slice. The times are simulated.
256 devices in a mesh: row: 16 (over x, y), ka: 16 (over z, core).
Axes of the slice: x: 4, y: 4, z: 8, core: 2. Of those that a mesh axis runs over, the one named last changes fastest.
Arguments:
- t2: bfloat16 [16, 4096, 128], P('row', 'ka'), may hold values from -6 to 6
- vtiles: bfloat16 [16, 16, 160, 128, 128], P('row', 'ka'), may hold values from -0.078125 to 0.078125
- need_cd: int32 [16, 16, 64], P(None, 'ka'), may hold values from 0 to 255, as said below
- tile_cd: int32 [16, 16, 160], P('row', 'ka'), may hold values from 0 to 63
- tile_ab: int32 [16, 16, 160], P('row', 'ka'), may hold values from 0 to 63
Outputs:
- ladder: bfloat16 [1024, 16, 128], P(('row', 'ka'))
Inputs may be any that keep to these rules, and one draw needn't show every extreme that they name: `need_cd`: the 64 entries of one block's list are all different.
All inputs are finite; a program needn't handle non-finite values.
Results may differ from a plain program's by a relative error of at most 0.0015.
Values may be sent and summed in bfloat16 or wider, within the bound.
No kernel may reach another device: no remote copies, remote signals or barrier semaphores. Data moves between devices by JAX's collectives and lax.ppermute only.
A program may use at most 64 MiB of HBM per device.

v0:
```python
import jax
import jax.numpy as jnp
from jax import lax
from jax.sharding import PartitionSpec as P

AB_DEV = 64


def on_device(t2, vtiles, need_cd, tile_cd, tile_ab):
    pairs_all = t2.shape[0] * lax.axis_size("row")
    tile_edge = t2.shape[2]
    slot_cd = tile_cd[0, 0]
    slot_ab = tile_ab[0, 0]
    blocks = vtiles[0, 0]
    slot_count = slot_cd.shape[0]
    own_list = lax.dynamic_index_in_dim(need_cd[:, 0, :], lax.axis_index("row"), 0, keepdims=False)
    whole = lax.all_gather(t2, "row", axis=0, tiled=True)
    picked = jnp.take(whole, own_list[slot_cd], axis=1)
    products = jnp.einsum("pst,stu->spu", picked, blocks, preferred_element_type=jnp.float32)
    products = products.reshape(slot_count, pairs_all * tile_edge)
    upper_part = lax.optimization_barrier(products.astype(jnp.bfloat16))
    lower_part = (products - upper_part.astype(jnp.float32)).astype(jnp.bfloat16)
    share = AB_DEV // lax.axis_size("ka")
    wanted_rows = lax.iota(jnp.int32, share * lax.axis_size("ka"))
    onehot = (slot_ab[None, :] == wanted_rows[:, None]).astype(jnp.bfloat16)
    summed = jnp.dot(onehot, upper_part, preferred_element_type=jnp.float32)
    summed = summed + jnp.dot(onehot, lower_part, preferred_element_type=jnp.float32)
    reduced = lax.psum_scatter(
        summed.reshape(share * lax.axis_size("ka"), pairs_all, tile_edge),
        "ka",
        scatter_dimension=0,
        tiled=True,
    )
    return reduced.astype(jnp.bfloat16)


def solution(mesh):
    return jax.shard_map(
        on_device,
        mesh=mesh,
        in_specs=(
            P("row", "ka", None),
            P("row", "ka", None, None, None),
            P(None, "ka", None),
            P("row", "ka", None),
            P("row", "ka", None),
        ),
        out_specs=P(("row", "ka"), None, None),
        check_vma=False,
    )
```

profile of v0, /device:TPU:1, one launch (start us, length us, event | category | flops | bytes accessed | tf_op | source)
XLA Modules:
  0.0 131.9 jit_solution(1743452980378425177)
XLA Ops:
  6.5 0.0 copy-start
  6.5 0.0 all-gather.2.cloned.1.call-start
  6.5 0.7 all-gather.2.cloned.1.call-update
  7.3 0.0 reduce-scatter.2.cloned.1.call-start
  7.3 0.0 copy-done
  7.3 0.7 compare_select_fusion.1
  8.0 1.5 %gather_fusion = s32[160]{0:T(256)S(1)} fusion(s32[64]{0:T(128)S(1)} %dynamic-slice_bitcast_fusion, s32[1024]{0:T(1024)S(1)} %pad_clamp_fusion.1), kind=kCustom, calls=%fused_computation | custom fusion | bytes 1920 | tf_op jit(solution)/shard_map/gather | solution.py:18
  9.6 49.7 %all-gather.2.cloned.1.call-done = bf16[16,256,128]{2,1,0:T(8,128)(2,1)} async-done(((bf16[1,256,128]{2,1,0:T(8,128)(2,1)}), bf16[16,256,128]{2,1,0:T(8,128)(2,1)}) %all-gather.2.cloned.1.call-update) | async-done | bytes 1048592 | tf_op jit(solution)/shard_map/all_gather | solution.py:17
  59.3 1.9 %copy.8 = bf16[16,256,128]{2,0,1:T(8,128)(2,1)S(1)} copy(bf16[16,256,128]{2,1,0:T(8,128)(2,1)} %all-gather.2.cloned.1.call-done) | data formatting | bytes 2097152 | tf_op jit(solution)/shard_map/all_gather | solution.py:17
  61.2 0.7 gather_fusion.1
  61.9 3.5 %fusion = f32[160,16,128]{2,1,0:T(8,128)S(1)} fusion(bf16[1,1,160,128,128]{4,3,2,1,0:T(8,128)(2,1)} %param.6, bf16[160,16,128]{2,1,0:T(8,128)(2,1)S(1)} %gather_fusion.1, pred[160]{0:T(512)(128)(4,1)S(1)} %compare_and_fusion), kind=kOutput, calls=%fused_computation.2 | convolution fusion | flops 84213760 | bytes 7209120 | tf_op jit(solution)/shard_map/pst,stu->spu/dot_general | solution.py:19
  65.4 0.0 copy-start.1
  65.4 0.5 copy.14
  66.0 0.2 copy-done.1
  66.1 0.2 fusion.9
  66.4 0.6 fusion.3
  66.9 0.9 copy.10
  67.8 0.0 reduce-scatter.2.cloned.1.call-update
  67.8 55.8 %reduce-scatter.2.cloned.1.call-done = f32[4,16,128]{2,1,0:T(8,128)} async-done(((f32[64,16,128]{2,1,0:T(8,128)}), f32[4,16,128]{2,1,0:T(8,128)}) %reduce-scatter.2.cloned.1.call-update) | async-done | bytes 32784 | tf_op jit(solution)/shard_map/reduce_scatter | solution.py:28
  123.6 1.4 %convert_element_type.16 = bf16[4,16,128]{2,1,0:T(8,128)(2,1)} convert(f32[4,16,128]{2,1,0:T(8,128)} %reduce-scatter.2.cloned.1.call-done) | non-fusion elementwise | flops 8192 | bytes 49152 | tf_op jit(solution)/shard_map/convert_element_type | solution.py:34
  (5 shorter events, 0.0 us)
Async XLA Ops:
  6.5 0.8 copy-start
  6.5 52.8 %all-gather.2.cloned.1.call-start = ((), (), s32[]{:S(2)}) async-start(), calls=%async_computation.1 | async-start | bytes 1114112 | tf_op jit(solution)/shard_map/all_gather | solution.py:17
  7.3 116.4 %reduce-scatter.2.cloned.1.call-start = ((), (), s32[]{:S(2)}) async-start(), calls=%async_computation.2 | async-start | bytes 557056 | tf_op jit(solution)/shard_map/reduce_scatter | solution.py:28
  65.4 0.7 copy-start.1
Sparse Core Ops, SparseCore 0:
  9.8 49.4 all-gather.1
  67.9 55.6 reduce-scatter.1
where the time goes:
time: 134 us; the launch traced here: 132 us
  waiting for transfers between devices  106 us (79%)
  between operations  13.5 us (10%)
  local copies, waits for them, and re-layouts  5.76 us (4%)
  matrix products  4.27 us (3%)
  other arithmetic  2.08 us (2%)
    reduce_scatter x1, waiting for transfers between devices, on_device(): lax.psum_scatter(summed.reshape(share * lax.axis_size('ka'), pairs_all, t...  55.8 us
    all_gather x1, waiting for transfers between devices, on_device(): whole = lax.all_gather(t2, 'row', axis=0, tiled=True)  49.7 us
    dot_general x1, matrix products, on_device(): jnp.einsum('pst,stu->spu', picked, blocks, preferred_element_type=jnp.flo...  3.47 us
  transfers between devices with their start and end apart: 2, of which 2 were waited for; matrix products, arithmetic and copies ran while one was open for 2% of the time, Pallas kernels for 0%

commit v1 on v0

v1 whole, which is shorter than its diff:
```python
import jax
import jax.numpy as jnp
from jax import lax
from jax.sharding import PartitionSpec as P

AB_DEV = 64


def gather_oh(t2, need_cd):
    lists = need_cd[:, 0, :]
    send = jnp.take(t2[0], lists, axis=0)
    return lax.all_to_all(send, "row", 0, 0, tiled=True)


def gather_pp(t2, need_cd):
    n = lax.axis_size("row")
    me = lax.axis_index("row")
    lists = need_cd[:, 0, :]
    own = lax.dynamic_index_in_dim(lists, me, 0, keepdims=False)
    parts = [None] * n
    parts[0] = jnp.take(t2[0], own, axis=0)
    for j in range(1, n):
        dest = (me + j) % n
        rows = lax.dynamic_index_in_dim(lists, dest, 0, keepdims=False)
        got = lax.ppermute(jnp.take(t2[0], rows, axis=0), "row", [(i, (i + j) % n) for i in range(n)])
        parts[j] = got
    stacked = jnp.stack(parts)
    src = (me - jnp.arange(n)) % n
    order = jnp.argsort(src)
    return jnp.take(stacked, order, axis=0)


def gather_ag(t2, need_cd):
    own = lax.dynamic_index_in_dim(need_cd[:, 0, :], lax.axis_index("row"), 0, keepdims=False)
    whole = lax.all_gather(t2, "row", axis=0, tiled=True)
    return jnp.take(whole, own, axis=1)


def reduce_rs(summed):
    return lax.psum_scatter(summed, "ka", scatter_dimension=0, tiled=True)


def reduce_h(summed):
    n = (lax.axis_size("z") * lax.axis_size("c"))
    s = summed.reshape(n, summed.shape[0] // n, *summed.shape[1:])
    got = lax.all_to_all(s, "ka", 0, 0, tiled=True)
    return got.sum(axis=0)


def reduce_pp(summed):
    n = (lax.axis_size("z") * lax.axis_size("c"))
    me = lax.axis_index("ka")
    share = summed.shape[0] // n
    s = summed.reshape(n, share, *summed.shape[1:])
    total = lax.dynamic_index_in_dim(s, me, 0, keepdims=False)
    for j in range(1, n):
        dest = (me + j) % n
        part = lax.dynamic_index_in_dim(s, dest, 0, keepdims=False)
        total = total + lax.ppermute(part, "ka", [(i, (i + j) % n) for i in range(n)])
    return total


def reduce_h(summed):
    nz = lax.axis_size("z")
    nc = lax.axis_size("c")
    share = summed.shape[0] // (nz * nc)
    s = summed.reshape(nz, nc, share, *summed.shape[1:])
    got = lax.all_to_all(s, "c", 1, 1, tiled=True)
    s = got.sum(axis=1)
    got = lax.all_to_all(s, "z", 0, 0, tiled=True)
    return got.sum(axis=0)


def gather_oh(t2, need_cd):
    lists = need_cd[:, 0, :]
    n_rows = t2.shape[1]
    onehot = (lists.reshape(-1)[:, None] == lax.iota(jnp.int32, n_rows)[None, :]).astype(t2.dtype)
    send = jnp.dot(onehot, t2[0], preferred_element_type=jnp.float32).astype(t2.dtype)
    send = send.reshape(lists.shape[0], lists.shape[1], t2.shape[2])
    return lax.all_to_all(send, "row", 0, 0, tiled=True)


def on_device(t2, vtiles, need_cd, tile_cd, tile_ab):
    pairs_all = t2.shape[0] * lax.axis_size("row")
    tile_edge = t2.shape[2]
    slot_cd = tile_cd[0, 0]
    slot_ab = tile_ab[0, 0]
    blocks = vtiles[0, 0]
    slot_count = slot_cd.shape[0]
    mine = gather_oh(t2, need_cd)
    picked = jnp.take(mine, slot_cd, axis=1)
    products = jnp.einsum("pst,stu->spu", picked, blocks, preferred_element_type=jnp.float32)
    products = products.reshape(slot_count, pairs_all * tile_edge)
    upper_part = lax.optimization_barrier(products.astype(jnp.bfloat16))
    lower_part = (products - upper_part.astype(jnp.float32)).astype(jnp.bfloat16)
    share = AB_DEV // (lax.axis_size("z") * lax.axis_size("c"))
    wanted_rows = lax.iota(jnp.int32, share * (lax.axis_size("z") * lax.axis_size("c")))
    onehot = (slot_ab[None, :] == wanted_rows[:, None]).astype(jnp.bfloat16)
    summed = jnp.dot(onehot, upper_part, preferred_element_type=jnp.float32)
    summed = summed + jnp.dot(onehot, lower_part, preferred_element_type=jnp.float32)
    reduced = reduce_h(summed.reshape(share * (lax.axis_size("z") * lax.axis_size("c")), pairs_all, tile_edge))
    return reduced.astype(jnp.bfloat16)


def solution(mesh):
    from jax.sharding import Mesh
    devs = mesh.devices
    n_ka = devs.shape[1]
    fine = Mesh(devs.reshape(devs.shape[0], n_ka // 2, 2), ("row", "z", "c"))
    return jax.shard_map(
        on_device,
        mesh=fine,
        in_specs=(
            P("row", ("z", "c"), None),
            P("row", ("z", "c"), None, None, None),
            P(None, ("z", "c"), None),
            P("row", ("z", "c"), None),
            P("row", ("z", "c"), None),
        ),
        out_specs=P(("row", "z", "c"), None, None),
        check_vma=False,
    )
```

time: 134 us -> 50 us (0.37); the launches traced: 132 us -> 49.6 us
  waiting for transfers between devices: 106 us -> 6.08 us
  blocking collectives: 0 us -> 24.9 us
  between operations: 13.5 us -> 0.07 us
  starting transfers between devices: 0.04 us -> 7.57 us
  local copies, waits for them, and re-layouts: 5.76 us -> 2.3 us
    reduce_scatter x1 -> x0, waiting for transfers between devices: 55.8 us -> none  [on_device(): lax.psum_scatter(summed.reshape(share * lax.axis_size('ka'), pairs_all, t...]
    all_gather x1 -> x0, waiting for transfers between devices: 49.7 us -> none  [on_device(): whole = lax.all_gather(t2, 'row', axis=0, tiled=True)]
    all_to_all x0 -> x2, blocking collectives: none -> 24.9 us  [the longest x1 19.1 us: reduce_h(): got = lax.all_to_all(s, 'z', 0, 0, tiled=True)]
    all_to_all x0 -> x1, starting transfers between devices: none -> 7.57 us  [gather_oh(): return lax.all_to_all(send, 'row', 0, 0, tiled=True)]
    all_to_all x0 -> x1, waiting for transfers between devices: none -> 6.08 us  [gather_oh(): return lax.all_to_all(send, 'row', 0, 0, tiled=True)]
    all_gather x1 -> x0, local copies, waits for them, and re-layouts: 1.9 us -> none  [on_device(): whole = lax.all_gather(t2, 'row', axis=0, tiled=True)]
    gather x2 -> x1, local copies, waits for them, and re-layouts: 2.29 us -> 0.74 us  [on_device(): picked = jnp.take(mine, slot_cd, axis=1)]
    unnamed x0 -> x1, other arithmetic: none -> 1.37 us
  transfers between devices with their start and end apart: 2 -> 1, of which waited for: 2 -> 1; matrix products, arithmetic and copies ran while one was open for 2% -> 3% of each run, Pallas kernels for 0% -> 0%
where the time goes in v1:
time: 50 us; the launch traced here: 49.6 us
  blocking collectives  24.9 us (50%)
  starting transfers between devices  7.57 us (15%)
  waiting for transfers between devices  6.08 us (12%)
  matrix products  5.31 us (11%)
  other arithmetic  3.4 us (7%)
  local copies, waits for them, and re-layouts  2.3 us (5%)
    all_to_all x1, blocking collectives, reduce_h(): got = lax.all_to_all(s, 'z', 0, 0, tiled=True)  19.1 us
    all_to_all x1, starting transfers between devices, gather_oh(): return lax.all_to_all(send, 'row', 0, 0, tiled=True)  7.57 us
    all_to_all x1, waiting for transfers between devices, gather_oh(): return lax.all_to_all(send, 'row', 0, 0, tiled=True)  6.08 us
    all_to_all x1, blocking collectives, reduce_h(): got = lax.all_to_all(s, 'c', 1, 1, tiled=True)  5.8 us
    dot_general x1, matrix products, on_device(): jnp.einsum('pst,stu->spu', picked, blocks, preferred_element_type=jnp.flo...  3.47 us
    unnamed x1, other arithmetic  1.37 us
    unnamed x7, local copies, waits for them, and re-layouts  1.28 us
    dot_general x1, matrix products, gather_oh(): jnp.dot(onehot, t2[0], preferred_element_type=jnp.float32).astype(t2.dtype)  1.05 us
  transfers between devices with their start and end apart: 1, of which 1 were waited for; matrix products, arithmetic and copies ran while one was open for 3% of the time, Pallas kernels for 0%

profile of v1, /device:TPU:1, one launch (start us, length us, event | category | flops | bytes accessed | tf_op | source)
XLA Modules:
  0.0 49.6 jit_solution(17539781590661634732)
XLA Ops:
  0.0 0.0 copy-start
  0.0 0.5 %broadcast.42 = s32[]{:T(128)} broadcast(s32[]{:T(128)} %constant.42), dimensions={} | broadcast | bytes 8 | tf_op args[2]
  0.5 1.4 %reduce.3 = s32[16,64]{1,0:T(8,128)S(1)} reduce(s32[16,1,64]{2,1,0:T(1,128)} %param.7, s32[]{:T(128)} %broadcast.42), dimensions={1}, to_apply=%param.7.reduce_sub_computation.3 | reduce | bytes 8196 | tf_op args[2]
  1.9 0.1 eq.34
  2.0 0.0 copy-done
  2.0 1.1 %convolution_convert_fusion = bf16[1024,128]{1,0:T(8,128)(2,1)} fusion(s32[1024]{0:T(1024)S(1)} %eq.34, bf16[1,256,128]{2,1,0:T(8,128)(2,1)S(1)} %copy-done), kind=kOutput, calls=%fused_computation.8 | convolution fusion | flops 67502080 | bytes 331776 | tf_op jit(solution)/shard_map/dot_general | solution.py:78
  3.0 7.6 %all-to-all-start = ((bf16[16,64,128]{2,1,0:T(8,128)(2,1)}), bf16[16,64,128]{2,1,0:T(8,128)(2,1)S(1)}, u32[]{:S(2)}, u32[]{:S(2)}) async-start(bf16[16,64,128]{2,1,0:T(8,128)(2,1)} %bitcast.3), calls=%async_computation | async-start | bytes 524288 | tf_op jit(solution)/shard_map/all_to_all | solution.py:80
  10.6 0.7 %compare_select_fusion = s32[160,1]{0,1:T(1,128)S(1)} fusion(s32[1,1,160]{2,1,0:T(1,128)} %param.8), kind=kLoop, calls=%fused_computation.20 | loop fusion | flops 480 | bytes 1280 | tf_op jit(solution)/shard_map/jit(_take)/jit(_where)/select_n | solution.py:91
  11.3 0.7 %compare_and_fusion = pred[160]{0:T(512)(128)(4,1)S(1)} fusion(s32[160]{0:T(256)} %bitcast.36), kind=kLoop, calls=%fused_computation.23 | loop fusion | flops 960 | bytes 800 | tf_op jit(solution)/shard_map/jit(_take)/and | solution.py:91
  12.0 6.1 %all-to-all-done = bf16[16,64,128]{2,1,0:T(8,128)(2,1)S(1)} async-done(((bf16[16,64,128]{2,1,0:T(8,128)(2,1)}), bf16[16,64,128]{2,1,0:T(8,128)(2,1)S(1)}, u32[]{:S(2)}, u32[]{:S(2)}) %all-to-all-start) | async-done | bytes 262176 | tf_op jit(solution)/shard_map/all_to_all | solution.py:80
  18.0 0.2 copy.9
  18.2 0.7 %gather_fusion = bf16[160,16,128]{2,1,0:T(8,128)(2,1)S(1)} fusion(bf16[16,64,128]{2,0,1:T(8,128)(2,1)S(1)} %copy.9, s32[1024]{0:T(1024)S(1)} %pad_clamp_fusion), kind=kCustom, calls=%fused_computation | custom fusion | bytes 1311360 | tf_op jit(solution)/shard_map/jit(_take)/gather | solution.py:91
  19.0 3.5 %fusion = f32[160,16,128]{2,1,0:T(8,128)S(1)} fusion(bf16[1,1,160,128,128]{4,3,2,1,0:T(8,128)(2,1)} %param.6, bf16[160,16,128]{2,1,0:T(8,128)(2,1)S(1)} %gather_fusion, pred[160]{0:T(512)(128)(4,1)S(1)} %compare_and_fusion), kind=kOutput, calls=%fused_computation.1 | convolution fusion | flops 84213760 | bytes 7209120 | tf_op jit(solution)/shard_map/pst,stu->spu/dot_general | solution.py:92
  22.4 0.0 copy-start.1
  22.5 0.5 %copy.16 = bf16[20,8,16,128]{3,1,2,0:T(8,128)(2,1)S(1)} copy(f32[20,8,16,128]{3,2,1,0:T(8,128)S(1)} %bitcast.28) | data formatting | bytes 1966080
  23.0 0.2 copy-done.1
  23.1 0.2 fusion.11
  23.4 0.6 %fusion.3 = f32[8,8,16,128]{3,1,2,0:T(8,128)S(1)} fusion(f32[64,2048]{1,0:T(8,128)S(1)} %fusion.11, bf16[160,2048]{1,0:T(8,128)(2,1)S(1)} %bitcast.31, f32[20,8,16,128]{3,2,1,0:T(8,128)S(1)} %bitcast.29, s32[160]{0:T(256)S(1)} %bitcast.35), kind=kOutput, calls=%fused_computation.7 | convolution fusion | flops 43067392 | bytes 3015296 | tf_op jit(solution)/shard_map/dot_general | solution.py:100
  23.9 0.1 copy.12
  24.1 5.8 %all_to_all.15 = f32[8,2,4,16,128]{4,3,2,0,1:T(8,128)S(1)} all-to-all(f32[8,2,4,16,128]{4,3,2,0,1:T(8,128)S(1)} %copy.10), channel_id=1, replica_groups=mesh['row'=16,'z'=8,'c'=2] {'c'}, dimensions={1} | all-to-all | bytes 1048576 | tf_op jit(solution)/shard_map/all_to_all | solution.py:68
  29.9 19.1 %all_to_all.16 = f32[8,4,16,128]{3,2,1,0:T(8,128)S(1)} all-to-all(f32[8,4,16,128]{3,2,1,0:T(8,128)S(1)} %reduce_sum.18), channel_id=1, replica_groups=mesh['row'=16,'z'=8,'c'=2] {'z'}, dimensions={0} | all-to-all | bytes 524288 | tf_op jit(solution)/shard_map/all_to_all | solution.py:70
  49.0 0.6 %reduce_sum.19 = bf16[4,16,128]{2,1,0:T(8,128)(2,1)} reduce(f32[8,4,16,128]{3,2,1,0:T(8,128)S(1)} %all_to_all.16, f32[]{:T(128)} %constant.17.clone.1), dimensions={0}, to_apply=%region_1.2 | reduce | flops 57344 | bytes 278532 | tf_op jit(solution)/shard_map/reduce_sum | solution.py:71
  (3 shorter events, 0.1 us)
Async XLA Ops:
  0.0 2.0 %copy-start = (bf16[1,256,128]{2,1,0:T(8,128)(2,1)S(1)}, bf16[1,256,128]{2,1,0:T(8,128)(2,1)}, u32[]{:S(2)}) copy-start(bf16[1,256,128]{2,1,0:T(8,128)(2,1)} %param.5) | copy-start | bytes 196612
  3.0 15.0 %all-to-all-start = ((bf16[16,64,128]{2,1,0:T(8,128)(2,1)}), bf16[16,64,128]{2,1,0:T(8,128)(2,1)S(1)}, u32[]{:S(2)}, u32[]{:S(2)}) async-start(bf16[16,64,128]{2,1,0:T(8,128)(2,1)} %bitcast.3), calls=%async_computation | async-start | bytes 524288 | tf_op jit(solution)/shard_map/all_to_all | solution.py:80
  22.4 0.7 %copy-start.1 = (s32[1,1,160]{2,1,0:T(1,128)S(1)}, s32[1,1,160]{2,1,0:T(1,128)}, u32[]{:S(2)}) copy-start(s32[1,1,160]{2,1,0:T(1,128)} %param.9) | copy-start | bytes 1924

commit v2 on v1

--- a/solution.py
+++ b/solution.py
@@ -72,11 +72,9 @@
 
 
 def gather_oh(t2, need_cd):
-    lists = need_cd[:, 0, :]
     n_rows = t2.shape[1]
-    onehot = (lists.reshape(-1)[:, None] == lax.iota(jnp.int32, n_rows)[None, :]).astype(t2.dtype)
-    send = jnp.dot(onehot, t2[0], preferred_element_type=jnp.float32).astype(t2.dtype)
-    send = send.reshape(lists.shape[0], lists.shape[1], t2.shape[2])
+    onehot = (need_cd[..., None] == lax.iota(jnp.int32, n_rows)).astype(t2.dtype)
+    send = jnp.einsum("dkqc,kct->dqt", onehot, t2, preferred_element_type=jnp.float32).astype(t2.dtype)
     return lax.all_to_all(send, "row", 0, 0, tiled=True)
 
 

time: 50 us -> 48.9 us (0.978)
  other arithmetic: 3.4 us -> 0.68 us
  waiting for transfers between devices: 6.08 us -> 7.4 us
  local copies, waits for them, and re-layouts: 2.3 us -> 3.32 us
  matrix products: 5.31 us -> 4.61 us
    unnamed x1 -> x0, other arithmetic: 1.37 us -> none
    all_to_all x1, waiting for transfers between devices: 6.08 us -> 7.4 us  [gather_oh(): return lax.all_to_all(send, 'row', 0, 0, tiled=True)]
    convert_element_type x0 -> x1, local copies, waits for them, and re-layouts: none -> 0.76 us  [gather_oh(): jnp.einsum('dkqc,kct->dqt', onehot, t2, preferred_element_type=jnp.float32)]
    eq x1, local copies, waits for them, and re-layouts: 0.07 us -> 0.81 us  [gather_oh(): need_cd[..., None] == lax.iota(jnp.int32, n_rows)]
    dot_general x1, matrix products: 1.05 us -> 0.35 us  [gather_oh(): jnp.einsum('dkqc,kct->dqt', onehot, t2, preferred_element_type=jnp.float32)]
    select_n x1, other arithmetic: 0.68 us -> 0.01 us  [on_device(): picked = jnp.take(mine, slot_cd, axis=1)]
    and x1, other arithmetic: 0.68 us -> 0.01 us  [on_device(): picked = jnp.take(mine, slot_cd, axis=1)]
    unnamed x7 -> x8, local copies, waits for them, and re-layouts: 1.28 us -> 0.79 us
  transfers between devices with their start and end apart: 1 -> 1, of which waited for: 1 -> 1; matrix products, arithmetic and copies ran while one was open for 3% -> 0% of each run, Pallas kernels for 0% -> 0%
where the time goes in v2:
time: 48.9 us; the launch traced here: 48.6 us
  blocking collectives  24.9 us (51%)
  starting transfers between devices  7.57 us (15%)
  waiting for transfers between devices  7.4 us (15%)
  matrix products  4.61 us (9%)
  local copies, waits for them, and re-layouts  3.32 us (7%)
  other arithmetic  0.68 us (1%)
    all_to_all x1, blocking collectives, reduce_h(): got = lax.all_to_all(s, 'z', 0, 0, tiled=True)  19.1 us
    all_to_all x1, starting transfers between devices, gather_oh(): return lax.all_to_all(send, 'row', 0, 0, tiled=True)  7.57 us
    all_to_all x1, waiting for transfers between devices, gather_oh(): return lax.all_to_all(send, 'row', 0, 0, tiled=True)  7.4 us
    all_to_all x1, blocking collectives, reduce_h(): got = lax.all_to_all(s, 'c', 1, 1, tiled=True)  5.81 us
    dot_general x1, matrix products, on_device(): jnp.einsum('pst,stu->spu', picked, blocks, preferred_element_type=jnp.flo...  3.47 us
  transfers between devices with their start and end apart: 1, of which 1 were waited for; matrix products, arithmetic and copies ran while one was open for 0% of the time, Pallas kernels for 0%

profile of v2, /device:TPU:1, one launch (start us, length us, event | category | flops | bytes accessed | tf_op | source)
XLA Modules:
  0.0 48.6 jit_solution(13602372605503569140)
XLA Ops:
  0.0 0.0 copy-start
  0.0 0.0 copy-start.2
  0.0 0.8 %copy.10 = s32[16,64]{0,1:T(8,128)S(1)} copy(s32[16,64]{1,0:T(8,128)} %bitcast.34) | data formatting | bytes 8192 | tf_op jit(solution)/shard_map/eq | solution.py:76
  0.8 0.0 copy-done
  0.8 0.4 convolution_convert_fusion
  1.2 0.8 %copy.11 = bf16[16,64,128]{2,1,0:T(8,128)(2,1)} copy(bf16[16,64,128]{2,0,1:T(8,128)(2,1)S(1)} %convolution_convert_fusion) | data formatting | bytes 524288 | tf_op jit(solution)/shard_map/convert_element_type | solution.py:77
  2.0 7.6 %all-to-all-start = ((bf16[16,64,128]{2,1,0:T(8,128)(2,1)}), bf16[16,64,128]{2,1,0:T(8,128)(2,1)S(1)}, u32[]{:S(2)}, u32[]{:S(2)}) async-start(bf16[16,64,128]{2,1,0:T(8,128)(2,1)} %copy.11), calls=%async_computation | async-start | bytes 524288 | tf_op jit(solution)/shard_map/all_to_all | solution.py:78
  9.5 0.0 copy-done.2
  9.6 7.4 %all-to-all-done = bf16[16,64,128]{2,1,0:T(8,128)(2,1)S(1)} async-done(((bf16[16,64,128]{2,1,0:T(8,128)(2,1)}), bf16[16,64,128]{2,1,0:T(8,128)(2,1)S(1)}, u32[]{:S(2)}, u32[]{:S(2)}) %all-to-all-start) | async-done | bytes 262176 | tf_op jit(solution)/shard_map/all_to_all | solution.py:78
  17.0 0.2 copy.12
  17.2 0.7 %gather_fusion = bf16[160,16,128]{2,1,0:T(8,128)(2,1)S(1)} fusion(bf16[16,64,128]{2,0,1:T(8,128)(2,1)S(1)} %copy.12, s32[1024]{0:T(1024)S(1)} %pad_clamp_fusion), kind=kCustom, calls=%fused_computation | custom fusion | bytes 1311360 | tf_op jit(solution)/shard_map/jit(_take)/gather | solution.py:89
  17.9 3.5 %fusion = f32[160,16,128]{2,1,0:T(8,128)S(1)} fusion(bf16[1,1,160,128,128]{4,3,2,1,0:T(8,128)(2,1)} %param.6, bf16[160,16,128]{2,1,0:T(8,128)(2,1)S(1)} %gather_fusion, pred[160]{0:T(512)(128)(4,1)S(1)} %compare_and_fusion), kind=kOutput, calls=%fused_computation.1 | convolution fusion | flops 84213760 | bytes 7209120 | tf_op jit(solution)/shard_map/pst,stu->spu/dot_general | solution.py:90
  21.4 0.0 copy-start.1
  21.4 0.5 %copy.19 = bf16[20,8,16,128]{3,1,2,0:T(8,128)(2,1)S(1)} copy(f32[20,8,16,128]{3,2,1,0:T(8,128)S(1)} %bitcast.29) | data formatting | bytes 1966080
  21.9 0.2 copy-done.1
  22.1 0.2 fusion.11
  22.3 0.6 %fusion.3 = f32[8,8,16,128]{3,1,2,0:T(8,128)S(1)} fusion(f32[64,2048]{1,0:T(8,128)S(1)} %fusion.11, bf16[160,2048]{1,0:T(8,128)(2,1)S(1)} %bitcast.32, f32[20,8,16,128]{3,2,1,0:T(8,128)S(1)} %bitcast.30, s32[160]{0:T(256)S(1)} %bitcast.37), kind=kOutput, calls=%fused_computation.7 | convolution fusion | flops 43067392 | bytes 3015296 | tf_op jit(solution)/shard_map/dot_general | solution.py:98
  22.9 0.1 copy.15
  23.0 5.8 %all_to_all.15 = f32[8,2,4,16,128]{4,3,2,0,1:T(8,128)S(1)} all-to-all(f32[8,2,4,16,128]{4,3,2,0,1:T(8,128)S(1)} %copy.13), channel_id=1, replica_groups=mesh['row'=16,'z'=8,'c'=2] {'c'}, dimensions={1} | all-to-all | bytes 1048576 | tf_op jit(solution)/shard_map/all_to_all | solution.py:68
  28.9 19.1 %all_to_all.16 = f32[8,4,16,128]{3,2,1,0:T(8,128)S(1)} all-to-all(f32[8,4,16,128]{3,2,1,0:T(8,128)S(1)} %reduce_sum.18), channel_id=1, replica_groups=mesh['row'=16,'z'=8,'c'=2] {'z'}, dimensions={0} | all-to-all | bytes 524288 | tf_op jit(solution)/shard_map/all_to_all | solution.py:70
  48.0 0.6 %reduce_sum.19 = bf16[4,16,128]{2,1,0:T(8,128)(2,1)} reduce(f32[8,4,16,128]{3,2,1,0:T(8,128)S(1)} %all_to_all.16, f32[]{:T(128)} %constant.17.clone.1), dimensions={0}, to_apply=%region_1.2 | reduce | flops 57344 | bytes 278532 | tf_op jit(solution)/shard_map/reduce_sum | solution.py:71
  (5 shorter events, 0.1 us)
Async XLA Ops:
  0.0 0.8 %copy-start = (bf16[1,256,128]{2,1,0:T(8,128)(2,1)S(1)}, bf16[1,256,128]{2,1,0:T(8,128)(2,1)}, u32[]{:S(2)}) copy-start(bf16[1,256,128]{2,1,0:T(8,128)(2,1)} %param.5) | copy-start | bytes 196612
  0.0 9.5 %copy-start.2 = (s32[1,1,160]{2,1,0:T(1,128)S(1)}, s32[1,1,160]{2,1,0:T(1,128)}, u32[]{:S(2)}) copy-start(s32[1,1,160]{2,1,0:T(1,128)} %param.8) | copy-start | bytes 1924
  2.0 15.0 %all-to-all-start = ((bf16[16,64,128]{2,1,0:T(8,128)(2,1)}), bf16[16,64,128]{2,1,0:T(8,128)(2,1)S(1)}, u32[]{:S(2)}, u32[]{:S(2)}) async-start(bf16[16,64,128]{2,1,0:T(8,128)(2,1)} %copy.11), calls=%async_computation | async-start | bytes 524288 | tf_op jit(solution)/shard_map/all_to_all | solution.py:78
  21.4 0.7 %copy-start.1 = (s32[1,1,160]{2,1,0:T(1,128)S(1)}, s32[1,1,160]{2,1,0:T(1,128)}, u32[]{:S(2)}) copy-start(s32[1,1,160]{2,1,0:T(1,128)} %param.9) | copy-start | bytes 1924

commit v3 on v2

--- a/solution.py
+++ b/solution.py
@@ -81,6 +81,8 @@
 def on_device(t2, vtiles, need_cd, tile_cd, tile_ab):
     pairs_all = t2.shape[0] * lax.axis_size("row")
     tile_edge = t2.shape[2]
+    nz, nc = lax.axis_size("z"), lax.axis_size("c")
+    share = AB_DEV // (nz * nc)
     slot_cd = tile_cd[0, 0]
     slot_ab = tile_ab[0, 0]
     blocks = vtiles[0, 0]
@@ -89,15 +91,20 @@
     picked = jnp.take(mine, slot_cd, axis=1)
     products = jnp.einsum("pst,stu->spu", picked, blocks, preferred_element_type=jnp.float32)
     products = products.reshape(slot_count, pairs_all * tile_edge)
+    owner = slot_ab // share
+    placed = (owner % nc) * (nz * share) + (owner // nc) * share + slot_ab % share
     upper_part = lax.optimization_barrier(products.astype(jnp.bfloat16))
     lower_part = (products - upper_part.astype(jnp.float32)).astype(jnp.bfloat16)
-    share = AB_DEV // (lax.axis_size("z") * lax.axis_size("c"))
-    wanted_rows = lax.iota(jnp.int32, share * (lax.axis_size("z") * lax.axis_size("c")))
-    onehot = (slot_ab[None, :] == wanted_rows[:, None]).astype(jnp.bfloat16)
+    onehot = (placed[None, :] == lax.iota(jnp.int32, AB_DEV)[:, None]).astype(jnp.bfloat16)
     summed = jnp.dot(onehot, upper_part, preferred_element_type=jnp.float32)
     summed = summed + jnp.dot(onehot, lower_part, preferred_element_type=jnp.float32)
-    reduced = reduce_h(summed.reshape(share * (lax.axis_size("z") * lax.axis_size("c")), pairs_all, tile_edge))
-    return reduced.astype(jnp.bfloat16)
+    s = summed.reshape(nc, nz, share, pairs_all, tile_edge)
+    me = lax.axis_index("c")
+    own = lax.dynamic_index_in_dim(s, me, 0, keepdims=False)
+    other = lax.dynamic_index_in_dim(s, 1 - me, 0, keepdims=False)
+    s = own + lax.ppermute(other, "c", [(0, 1), (1, 0)])
+    s = lax.all_to_all(s, "z", 0, 0, tiled=True).sum(axis=0)
+    return s.astype(jnp.bfloat16)
 
 
 def solution(mesh):

time: 48.9 us -> 46.2 us (0.945)
  blocking collectives: 24.9 us -> 19.1 us
  starting transfers between devices: 7.57 us -> 9.68 us
  waiting for transfers between devices: 7.4 us -> 8.52 us
    all_to_all x2 -> x1, blocking collectives: 24.9 us -> 19.1 us  [on_device(): s = lax.all_to_all(s, 'z', 0, 0, tiled=True).sum(axis=0)]
    ppermute x0 -> x1, starting transfers between devices: none -> 2.12 us  [on_device(): s = own + lax.ppermute(other, 'c', [(0, 1), (1, 0)])]
    ppermute x0 -> x1, waiting for transfers between devices: none -> 1.16 us  [on_device(): s = own + lax.ppermute(other, 'c', [(0, 1), (1, 0)])]
  transfers between devices with their start and end apart: 1 -> 2, of which waited for: 1 -> 2; matrix products, arithmetic and copies ran while one was open for 0% -> 0% of each run, Pallas kernels for 0% -> 0%
where the time goes in v3:
time: 46.2 us; the launch traced here: 45.9 us
  blocking collectives  19.1 us (41%)
  starting transfers between devices  9.68 us (21%)
  waiting for transfers between devices  8.52 us (18%)
  matrix products  4.62 us (10%)
  local copies, waits for them, and re-layouts  3.14 us (7%)
  other arithmetic  0.7 us (2%)
    all_to_all x1, blocking collectives, on_device(): s = lax.all_to_all(s, 'z', 0, 0, tiled=True).sum(axis=0)  19.1 us
    all_to_all x1, starting transfers between devices, gather_oh(): return lax.all_to_all(send, 'row', 0, 0, tiled=True)  7.57 us
    all_to_all x1, waiting for transfers between devices, gather_oh(): return lax.all_to_all(send, 'row', 0, 0, tiled=True)  7.36 us
    dot_general x1, matrix products, on_device(): jnp.einsum('pst,stu->spu', picked, blocks, preferred_element_type=jnp.flo...  3.48 us
    ppermute x1, starting transfers between devices, on_device(): s = own + lax.ppermute(other, 'c', [(0, 1), (1, 0)])  2.12 us
    ppermute x1, waiting for transfers between devices, on_device(): s = own + lax.ppermute(other, 'c', [(0, 1), (1, 0)])  1.16 us
  transfers between devices with their start and end apart: 2, of which 2 were waited for; matrix products, arithmetic and copies ran while one was open for 0% of the time, Pallas kernels for 0%

profile of v3, /device:TPU:1, one launch (start us, length us, event | category | flops | bytes accessed | tf_op | source)
XLA Modules:
  0.0 45.9 jit_solution(6179331214586636454)
XLA Ops:
  0.0 0.0 copy-start
  0.0 0.0 copy-start.1
  0.0 0.0 copy-start.2
  0.0 0.8 %copy.6 = s32[16,64]{0,1:T(8,128)S(1)} copy(s32[16,64]{1,0:T(8,128)} %bitcast.39) | data formatting | bytes 8192 | tf_op jit(solution)/shard_map/eq | solution.py:76
  0.8 0.0 copy-done
  0.8 0.4 convolution_convert_fusion
  1.2 0.8 %copy.7 = bf16[16,64,128]{2,1,0:T(8,128)(2,1)} copy(bf16[16,64,128]{2,0,1:T(8,128)(2,1)S(1)} %convolution_convert_fusion) | data formatting | bytes 524288 | tf_op jit(solution)/shard_map/convert_element_type | solution.py:77
  2.0 7.6 %all-to-all-start = ((bf16[16,64,128]{2,1,0:T(8,128)(2,1)}), bf16[16,64,128]{2,1,0:T(8,128)(2,1)S(1)}, u32[]{:S(2)}, u32[]{:S(2)}) async-start(bf16[16,64,128]{2,1,0:T(8,128)(2,1)} %copy.7), calls=%async_computation | async-start | bytes 524288 | tf_op jit(solution)/shard_map/all_to_all | solution.py:78
  9.5 0.0 copy-done.1
  9.6 0.0 copy-done.2
  9.6 7.4 %all-to-all-done = bf16[16,64,128]{2,1,0:T(8,128)(2,1)S(1)} async-done(((bf16[16,64,128]{2,1,0:T(8,128)(2,1)}), bf16[16,64,128]{2,1,0:T(8,128)(2,1)S(1)}, u32[]{:S(2)}, u32[]{:S(2)}) %all-to-all-start) | async-done | bytes 262176 | tf_op jit(solution)/shard_map/all_to_all | solution.py:78
  17.0 0.2 copy.8
  17.2 0.7 %gather_fusion = bf16[160,16,128]{2,1,0:T(8,128)(2,1)S(1)} fusion(bf16[16,64,128]{2,0,1:T(8,128)(2,1)S(1)} %copy.8, s32[1024]{0:T(1024)S(1)} %pad_clamp_fusion), kind=kCustom, calls=%fused_computation | custom fusion | bytes 1311360 | tf_op jit(solution)/shard_map/jit(_take)/gather | solution.py:91
  17.9 3.5 %fusion = f32[160,16,128]{2,1,0:T(8,128)S(1)} fusion(bf16[1,1,160,128,128]{4,3,2,1,0:T(8,128)(2,1)} %param.6, bf16[160,16,128]{2,1,0:T(8,128)(2,1)S(1)} %gather_fusion, pred[160]{0:T(512)(128)(4,1)S(1)} %compare_and_fusion), kind=kOutput, calls=%fused_computation.1 | convolution fusion | flops 84213760 | bytes 7209120 | tf_op jit(solution)/shard_map/pst,stu->spu/dot_general | solution.py:92
  21.4 0.5 %copy.14 = bf16[20,8,16,128]{3,1,2,0:T(8,128)(2,1)S(1)} copy(f32[20,8,16,128]{3,2,1,0:T(8,128)S(1)} %bitcast.33) | data formatting | bytes 1966080
  21.9 0.2 fusion.11
  22.1 0.6 %fusion.3 = f32[8,8,16,128]{3,1,2,0:T(8,128)S(1)} fusion(f32[64,2048]{1,0:T(8,128)S(1)} %fusion.11, bf16[160,2048]{1,0:T(8,128)(2,1)S(1)} %bitcast.36, f32[20,8,16,128]{3,2,1,0:T(8,128)S(1)} %bitcast.34, s32[160]{0:T(256)S(1)} %fusion.16), kind=kOutput, calls=%fused_computation.7 | convolution fusion | flops 43067392 | bytes 3015296 | tf_op jit(solution)/shard_map/dot_general | solution.py:100
  22.7 0.1 copy.10
  22.8 2.1 %collective-permute-start = (f32[8,4,16,128]{3,2,1,0:T(8,128)S(1)}, f32[8,4,16,128]{3,2,1,0:T(8,128)S(1)}, u32[]{:S(2)}, u32[]{:S(2)}) collective-permute-start(f32[8,4,16,128]{3,2,1,0:T(8,128)S(1)} %dynamic-slice_bitcast_fusion), channel_id=1, source_target_pairs={{0,1},{1,0},{2,3},{3,2},{4,5},{5,4},{6,7},{7,6},{8,9},{9,8},{10,11... | collective-permute-start | bytes 786440 | tf_op jit(solution)/shard_map/ppermute | solution.py:105
  25.0 1.2 %collective-permute-done = f32[8,4,16,128]{3,2,1,0:T(8,128)S(1)} collective-permute-done((f32[8,4,16,128]{3,2,1,0:T(8,128)S(1)}, f32[8,4,16,128]{3,2,1,0:T(8,128)S(1)}, u32[]{:S(2)}, u32[]{:S(2)}) %collective-permute-start) | collective-permute-done | bytes 262176 | tf_op jit(solution)/shard_map/ppermute | solution.py:105
  26.2 19.1 %all_to_all.10 = f32[8,4,16,128]{3,2,1,0:T(8,128)S(1)} all-to-all(f32[8,4,16,128]{3,2,1,0:T(8,128)S(1)} %bitcast_add_fusion), channel_id=1, replica_groups=mesh['row'=16,'z'=8,'c'=2] {'z'}, dimensions={0} | all-to-all | bytes 524288 | tf_op jit(solution)/shard_map/all_to_all | solution.py:106
  45.2 0.6 %reduce_sum.9 = bf16[4,16,128]{2,1,0:T(8,128)(2,1)} reduce(f32[8,4,16,128]{3,2,1,0:T(8,128)S(1)} %all_to_all.10, f32[]{:T(128)} %constant.76.clone.1), dimensions={0}, to_apply=%region_0.1 | reduce | flops 57344 | bytes 278532 | tf_op jit(solution)/shard_map/reduce_sum | solution.py:106
  (6 shorter events, 0.1 us)
Async XLA Ops:
  0.0 0.8 %copy-start = (bf16[1,256,128]{2,1,0:T(8,128)(2,1)S(1)}, bf16[1,256,128]{2,1,0:T(8,128)(2,1)}, u32[]{:S(2)}) copy-start(bf16[1,256,128]{2,1,0:T(8,128)(2,1)} %param.5) | copy-start | bytes 196612
  0.0 9.5 %copy-start.1 = (s32[1,1,160]{2,1,0:T(1,128)S(1)}, s32[1,1,160]{2,1,0:T(1,128)}, u32[]{:S(2)}) copy-start(s32[1,1,160]{2,1,0:T(1,128)} %param.8) | copy-start | bytes 1924
  0.0 9.6 %copy-start.2 = (s32[1,1,160]{2,1,0:T(1,128)S(1)}, s32[1,1,160]{2,1,0:T(1,128)}, u32[]{:S(2)}) copy-start(s32[1,1,160]{2,1,0:T(1,128)} %param.9) | copy-start | bytes 1924
  2.0 15.0 %all-to-all-start = ((bf16[16,64,128]{2,1,0:T(8,128)(2,1)}), bf16[16,64,128]{2,1,0:T(8,128)(2,1)S(1)}, u32[]{:S(2)}, u32[]{:S(2)}) async-start(bf16[16,64,128]{2,1,0:T(8,128)(2,1)} %copy.7), calls=%async_computation | async-start | bytes 524288 | tf_op jit(solution)/shard_map/all_to_all | solution.py:78
  22.8 3.3 %collective-permute-start = (f32[8,4,16,128]{3,2,1,0:T(8,128)S(1)}, f32[8,4,16,128]{3,2,1,0:T(8,128)S(1)}, u32[]{:S(2)}, u32[]{:S(2)}) collective-permute-start(f32[8,4,16,128]{3,2,1,0:T(8,128)S(1)} %dynamic-slice_bitcast_fusion), channel_id=1, source_target_pairs={{0,1},{1,0},{2,3},{3,2},{4,5},{5,4},{6,7},{7,6},{8,9},{9,8},{10,11... | collective-permute-start | bytes 786440 | tf_op jit(solution)/shard_map/ppermute | solution.py:105

commit v4 on v0

v4 whole, which is shorter than its diff:
```python
import functools

import jax
import jax.numpy as jnp
from jax import lax
from jax.experimental import pallas as pl
from jax.experimental.pallas import tpu as pltpu
from jax.sharding import Mesh
from jax.sharding import PartitionSpec as P

AB_DEV = 64


def gather_rows(t2, need_cd):
    n_rows = t2.shape[1]
    onehot = (need_cd[..., None] == lax.iota(jnp.int32, n_rows)).astype(t2.dtype)
    send = jnp.einsum("dkqc,kct->dqt", onehot, t2, preferred_element_type=jnp.float32).astype(t2.dtype)
    return lax.all_to_all(send, "row", 0, 0, tiled=True)


def reduce_rows(summed, nz, nc, share, pairs_all, tile_edge):
    s = summed.reshape(nc, nz, share, pairs_all, tile_edge)
    me = lax.axis_index("c")
    own = lax.dynamic_index_in_dim(s, me, 0, keepdims=False)
    other = lax.dynamic_index_in_dim(s, 1 - me, 0, keepdims=False)
    s = own + lax.ppermute(other, "c", [(0, 1), (1, 0)])
    s = lax.all_to_all(s, "z", 0, 0, tiled=True).sum(axis=0)
    return s.astype(jnp.bfloat16)


def on_device(t2, vtiles, need_cd, tile_cd, tile_ab):
    pairs_all = t2.shape[0] * lax.axis_size("row")
    tile_edge = t2.shape[2]
    nz, nc = lax.axis_size("z"), lax.axis_size("c")
    share = AB_DEV // (nz * nc)
    slot_cd = tile_cd[0, 0]
    slot_ab = tile_ab[0, 0]
    blocks = vtiles[0, 0]
    slot_count = slot_cd.shape[0]
    mine = gather_rows(t2, need_cd)
    picked = jnp.take(mine, slot_cd, axis=1)
    products = jnp.einsum("pst,stu->spu", picked, blocks, preferred_element_type=jnp.float32)
    products = products.reshape(slot_count, pairs_all * tile_edge)
    owner = slot_ab // share
    placed = (owner % nc) * (nz * share) + (owner // nc) * share + slot_ab % share
    upper_part = lax.optimization_barrier(products.astype(jnp.bfloat16))
    lower_part = (products - upper_part.astype(jnp.float32)).astype(jnp.bfloat16)
    onehot = (placed[None, :] == lax.iota(jnp.int32, AB_DEV)[:, None]).astype(jnp.bfloat16)
    summed = jnp.dot(onehot, upper_part, preferred_element_type=jnp.float32)
    summed = summed + jnp.dot(onehot, lower_part, preferred_element_type=jnp.float32)
    return reduce_rows(summed, nz, nc, share, pairs_all, tile_edge)


def solution(mesh):
    devs = mesh.devices
    n_ka = devs.shape[1]
    fine = Mesh(devs.reshape(devs.shape[0], n_ka // 2, 2), ("row", "z", "c"))
    cols = ("z", "c")
    return jax.shard_map(
        on_device,
        mesh=fine,
        in_specs=(
            P("row", cols, None),
            P("row", cols, None, None, None),
            P(None, cols, None),
            P("row", cols, None),
            P("row", cols, None),
        ),
        out_specs=P(("row", "z", "c"), None, None),
        check_vma=False,
    )
```

time: 134 us -> 46.2 us (0.34); the launches traced: 132 us -> 45.9 us
  waiting for transfers between devices: 106 us -> 8.52 us
  blocking collectives: 0 us -> 19.1 us
  between operations: 13.5 us -> 0.12 us
  starting transfers between devices: 0.04 us -> 9.68 us
  local copies, waits for them, and re-layouts: 5.76 us -> 3.15 us
  other arithmetic: 2.08 us -> 0.7 us
    reduce_scatter x1 -> x0, waiting for transfers between devices: 55.8 us -> none  [on_device(): lax.psum_scatter(summed.reshape(share * lax.axis_size('ka'), pairs_all, t...]
    all_gather x1 -> x0, waiting for transfers between devices: 49.7 us -> none  [on_device(): whole = lax.all_gather(t2, 'row', axis=0, tiled=True)]
    all_to_all x0 -> x1, blocking collectives: none -> 19.1 us  [reduce_rows(): s = lax.all_to_all(s, 'z', 0, 0, tiled=True).sum(axis=0)]
    all_to_all x0 -> x1, starting transfers between devices: none -> 7.57 us  [gather_rows(): return lax.all_to_all(send, 'row', 0, 0, tiled=True)]
    all_to_all x0 -> x1, waiting for transfers between devices: none -> 7.36 us  [gather_rows(): return lax.all_to_all(send, 'row', 0, 0, tiled=True)]
    ppermute x0 -> x1, starting transfers between devices: none -> 2.11 us  [reduce_rows(): s = own + lax.ppermute(other, 'c', [(0, 1), (1, 0)])]
    all_gather x1 -> x0, local copies, waits for them, and re-layouts: 1.9 us -> none  [on_device(): whole = lax.all_gather(t2, 'row', axis=0, tiled=True)]
    gather x2 -> x1, local copies, waits for them, and re-layouts: 2.29 us -> 0.74 us  [on_device(): picked = jnp.take(mine, slot_cd, axis=1)]
  transfers between devices with their start and end apart: 2 -> 2, of which waited for: 2 -> 2; matrix products, arithmetic and copies ran while one was open for 2% -> 0% of each run, Pallas kernels for 0% -> 0%
where the time goes in v4:
time: 46.2 us; the launch traced here: 45.9 us
  blocking collectives  19.1 us (41%)
  starting transfers between devices  9.68 us (21%)
  waiting for transfers between devices  8.52 us (18%)
  matrix products  4.63 us (10%)
  local copies, waits for them, and re-layouts  3.15 us (7%)
  other arithmetic  0.7 us (2%)
    all_to_all x1, blocking collectives, reduce_rows(): s = lax.all_to_all(s, 'z', 0, 0, tiled=True).sum(axis=0)  19.1 us
    all_to_all x1, starting transfers between devices, gather_rows(): return lax.all_to_all(send, 'row', 0, 0, tiled=True)  7.57 us
    all_to_all x1, waiting for transfers between devices, gather_rows(): return lax.all_to_all(send, 'row', 0, 0, tiled=True)  7.36 us
    dot_general x1, matrix products, on_device(): jnp.einsum('pst,stu->spu', picked, blocks, preferred_element_type=jnp.flo...  3.48 us
    ppermute x1, starting transfers between devices, reduce_rows(): s = own + lax.ppermute(other, 'c', [(0, 1), (1, 0)])  2.11 us
    ppermute x1, waiting for transfers between devices, reduce_rows(): s = own + lax.ppermute(other, 'c', [(0, 1), (1, 0)])  1.16 us
  transfers between devices with their start and end apart: 2, of which 2 were waited for; matrix products, arithmetic and copies ran while one was open for 0% of the time, Pallas kernels for 0%

profile of v4, /device:TPU:1, one launch (start us, length us, event | category | flops | bytes accessed | tf_op | source)
XLA Modules:
  0.0 45.9 jit_solution(6179331214586636454)
XLA Ops:
  0.0 0.0 copy-start
  0.0 0.0 copy-start.1
  0.0 0.0 copy-start.2
  0.0 0.8 %copy.6 = s32[16,64]{0,1:T(8,128)S(1)} copy(s32[16,64]{1,0:T(8,128)} %bitcast.39) | data formatting | bytes 8192 | tf_op jit(solution)/shard_map/eq | solution.py:16
  0.8 0.0 copy-done
  0.8 0.4 convolution_convert_fusion
  1.2 0.8 %copy.7 = bf16[16,64,128]{2,1,0:T(8,128)(2,1)} copy(bf16[16,64,128]{2,0,1:T(8,128)(2,1)S(1)} %convolution_convert_fusion) | data formatting | bytes 524288 | tf_op jit(solution)/shard_map/convert_element_type | solution.py:17
  2.0 7.6 %all-to-all-start = ((bf16[16,64,128]{2,1,0:T(8,128)(2,1)}), bf16[16,64,128]{2,1,0:T(8,128)(2,1)S(1)}, u32[]{:S(2)}, u32[]{:S(2)}) async-start(bf16[16,64,128]{2,1,0:T(8,128)(2,1)} %copy.7), calls=%async_computation | async-start | bytes 524288 | tf_op jit(solution)/shard_map/all_to_all | solution.py:18
  9.5 0.0 copy-done.1
  9.6 0.0 copy-done.2
  9.6 7.4 %all-to-all-done = bf16[16,64,128]{2,1,0:T(8,128)(2,1)S(1)} async-done(((bf16[16,64,128]{2,1,0:T(8,128)(2,1)}), bf16[16,64,128]{2,1,0:T(8,128)(2,1)S(1)}, u32[]{:S(2)}, u32[]{:S(2)}) %all-to-all-start) | async-done | bytes 262176 | tf_op jit(solution)/shard_map/all_to_all | solution.py:18
  17.0 0.2 copy.8
  17.2 0.7 %gather_fusion = bf16[160,16,128]{2,1,0:T(8,128)(2,1)S(1)} fusion(bf16[16,64,128]{2,0,1:T(8,128)(2,1)S(1)} %copy.8, s32[1024]{0:T(1024)S(1)} %pad_clamp_fusion), kind=kCustom, calls=%fused_computation | custom fusion | bytes 1311360 | tf_op jit(solution)/shard_map/jit(_take)/gather | solution.py:41
  17.9 3.5 %fusion = f32[160,16,128]{2,1,0:T(8,128)S(1)} fusion(bf16[1,1,160,128,128]{4,3,2,1,0:T(8,128)(2,1)} %param.6, bf16[160,16,128]{2,1,0:T(8,128)(2,1)S(1)} %gather_fusion, pred[160]{0:T(512)(128)(4,1)S(1)} %compare_and_fusion), kind=kOutput, calls=%fused_computation.1 | convolution fusion | flops 84213760 | bytes 7209120 | tf_op jit(solution)/shard_map/pst,stu->spu/dot_general | solution.py:42
  21.4 0.5 %copy.14 = bf16[20,8,16,128]{3,1,2,0:T(8,128)(2,1)S(1)} copy(f32[20,8,16,128]{3,2,1,0:T(8,128)S(1)} %bitcast.33) | data formatting | bytes 1966080
  21.9 0.2 fusion.11
  22.2 0.6 %fusion.3 = f32[8,8,16,128]{3,1,2,0:T(8,128)S(1)} fusion(f32[64,2048]{1,0:T(8,128)S(1)} %fusion.11, bf16[160,2048]{1,0:T(8,128)(2,1)S(1)} %bitcast.36, f32[20,8,16,128]{3,2,1,0:T(8,128)S(1)} %bitcast.34, s32[160]{0:T(256)S(1)} %fusion.16), kind=kOutput, calls=%fused_computation.7 | convolution fusion | flops 43067392 | bytes 3015296 | tf_op jit(solution)/shard_map/dot_general | solution.py:50
  22.7 0.1 copy.10
  22.8 2.1 %collective-permute-start = (f32[8,4,16,128]{3,2,1,0:T(8,128)S(1)}, f32[8,4,16,128]{3,2,1,0:T(8,128)S(1)}, u32[]{:S(2)}, u32[]{:S(2)}) collective-permute-start(f32[8,4,16,128]{3,2,1,0:T(8,128)S(1)} %dynamic-slice_bitcast_fusion), channel_id=1, source_target_pairs={{0,1},{1,0},{2,3},{3,2},{4,5},{5,4},{6,7},{7,6},{8,9},{9,8},{10,11... | collective-permute-start | bytes 786440 | tf_op jit(solution)/shard_map/ppermute | solution.py:26
  25.0 1.2 %collective-permute-done = f32[8,4,16,128]{3,2,1,0:T(8,128)S(1)} collective-permute-done((f32[8,4,16,128]{3,2,1,0:T(8,128)S(1)}, f32[8,4,16,128]{3,2,1,0:T(8,128)S(1)}, u32[]{:S(2)}, u32[]{:S(2)}) %collective-permute-start) | collective-permute-done | bytes 262176 | tf_op jit(solution)/shard_map/ppermute | solution.py:26
  26.2 19.1 %all_to_all.10 = f32[8,4,16,128]{3,2,1,0:T(8,128)S(1)} all-to-all(f32[8,4,16,128]{3,2,1,0:T(8,128)S(1)} %bitcast_add_fusion), channel_id=1, replica_groups=mesh['row'=16,'z'=8,'c'=2] {'z'}, dimensions={0} | all-to-all | bytes 524288 | tf_op jit(solution)/shard_map/all_to_all | solution.py:27
  45.2 0.6 %reduce_sum.9 = bf16[4,16,128]{2,1,0:T(8,128)(2,1)} reduce(f32[8,4,16,128]{3,2,1,0:T(8,128)S(1)} %all_to_all.10, f32[]{:T(128)} %constant.76.clone.1), dimensions={0}, to_apply=%region_0.1 | reduce | flops 57344 | bytes 278532 | tf_op jit(solution)/shard_map/reduce_sum | solution.py:27
  (6 shorter events, 0.1 us)
Async XLA Ops:
  0.0 0.8 %copy-start = (bf16[1,256,128]{2,1,0:T(8,128)(2,1)S(1)}, bf16[1,256,128]{2,1,0:T(8,128)(2,1)}, u32[]{:S(2)}) copy-start(bf16[1,256,128]{2,1,0:T(8,128)(2,1)} %param.5) | copy-start | bytes 196612
  0.0 9.5 %copy-start.1 = (s32[1,1,160]{2,1,0:T(1,128)S(1)}, s32[1,1,160]{2,1,0:T(1,128)}, u32[]{:S(2)}) copy-start(s32[1,1,160]{2,1,0:T(1,128)} %param.8) | copy-start | bytes 1924
  0.0 9.6 %copy-start.2 = (s32[1,1,160]{2,1,0:T(1,128)S(1)}, s32[1,1,160]{2,1,0:T(1,128)}, u32[]{:S(2)}) copy-start(s32[1,1,160]{2,1,0:T(1,128)} %param.9) | copy-start | bytes 1924
  2.0 15.0 %all-to-all-start = ((bf16[16,64,128]{2,1,0:T(8,128)(2,1)}), bf16[16,64,128]{2,1,0:T(8,128)(2,1)S(1)}, u32[]{:S(2)}, u32[]{:S(2)}) async-start(bf16[16,64,128]{2,1,0:T(8,128)(2,1)} %copy.7), calls=%async_computation | async-start | bytes 524288 | tf_op jit(solution)/shard_map/all_to_all | solution.py:18
  22.8 3.3 %collective-permute-start = (f32[8,4,16,128]{3,2,1,0:T(8,128)S(1)}, f32[8,4,16,128]{3,2,1,0:T(8,128)S(1)}, u32[]{:S(2)}, u32[]{:S(2)}) collective-permute-start(f32[8,4,16,128]{3,2,1,0:T(8,128)S(1)} %dynamic-slice_bitcast_fusion), channel_id=1, source_target_pairs={{0,1},{1,0},{2,3},{3,2},{4,5},{5,4},{6,7},{7,6},{8,9},{9,8},{10,11... | collective-permute-start | bytes 786440 | tf_op jit(solution)/shard_map/ppermute | solution.py:26

commit v5 on v4

--- a/solution.py
+++ b/solution.py
@@ -24,7 +24,12 @@
     own = lax.dynamic_index_in_dim(s, me, 0, keepdims=False)
     other = lax.dynamic_index_in_dim(s, 1 - me, 0, keepdims=False)
     s = own + lax.ppermute(other, "c", [(0, 1), (1, 0)])
-    s = lax.all_to_all(s, "z", 0, 0, tiled=True).sum(axis=0)
+    mz = lax.axis_index("z")
+    total = lax.dynamic_index_in_dim(s, mz, 0, keepdims=False)
+    for j in range(1, nz):
+        part = lax.dynamic_index_in_dim(s, (mz + j) % nz, 0, keepdims=False)
+        total = total + lax.ppermute(part, "z", [(i, (i + j) % nz) for i in range(nz)])
+    s = total
     return s.astype(jnp.bfloat16)
 
 

time: 46.2 us -> 45.6 us (0.987)
  blocking collectives: 19.1 us -> 0 us
  starting transfers between devices: 9.68 us -> 25 us
  waiting for transfers between devices: 8.52 us -> 11.4 us
    all_to_all x1 -> x0, blocking collectives: 19.1 us -> none  [reduce_rows(): s = lax.all_to_all(s, 'z', 0, 0, tiled=True).sum(axis=0)]
    ppermute x0 -> x7, starting transfers between devices: none -> 15.3 us  [reduce_rows(): lax.ppermute(part, 'z', [(i, (i + j) % nz) for i in range(nz)])]
    ppermute x0 -> x7, waiting for transfers between devices: none -> 2.89 us  [reduce_rows(): lax.ppermute(part, 'z', [(i, (i + j) % nz) for i in range(nz)])]
    reduce_sum x1 -> x0, other arithmetic: 0.62 us -> none  [reduce_rows(): s = lax.all_to_all(s, 'z', 0, 0, tiled=True).sum(axis=0)]
    convert_element_type x0 -> x1, other arithmetic: none -> 0.62 us  [reduce_rows(): return s.astype(jnp.bfloat16)]
  transfers between devices with their start and end apart: 2 -> 9, of which waited for: 2 -> 4; matrix products, arithmetic and copies ran while one was open for 0% -> 0% of each run, Pallas kernels for 0% -> 0%
where the time goes in v5:
time: 45.6 us; the launch traced here: 45 us
  starting transfers between devices  25 us (55%)
  waiting for transfers between devices  11.4 us (25%)
  matrix products  4.62 us (10%)
  local copies, waits for them, and re-layouts  3.18 us (7%)
  other arithmetic  0.7 us (2%)
    ppermute x7, starting transfers between devices, reduce_rows(): lax.ppermute(part, 'z', [(i, (i + j) % nz) for i in range(nz)])  15.3 us
    all_to_all x1, starting transfers between devices, gather_rows(): return lax.all_to_all(send, 'row', 0, 0, tiled=True)  7.57 us
    all_to_all x1, waiting for transfers between devices, gather_rows(): return lax.all_to_all(send, 'row', 0, 0, tiled=True)  7.36 us
    dot_general x1, matrix products, on_device(): jnp.einsum('pst,stu->spu', picked, blocks, preferred_element_type=jnp.flo...  3.48 us
    ppermute x7, waiting for transfers between devices, reduce_rows(): lax.ppermute(part, 'z', [(i, (i + j) % nz) for i in range(nz)])  2.89 us
    ppermute x1, starting transfers between devices, reduce_rows(): s = own + lax.ppermute(other, 'c', [(0, 1), (1, 0)])  2.12 us
    ppermute x1, waiting for transfers between devices, reduce_rows(): s = own + lax.ppermute(other, 'c', [(0, 1), (1, 0)])  1.16 us
  transfers between devices with their start and end apart: 9, of which 4 were waited for; matrix products, arithmetic and copies ran while one was open for 0% of the time, Pallas kernels for 0%

profile of v5, /device:TPU:1, one launch (start us, length us, event | category | flops | bytes accessed | tf_op | source)
XLA Modules:
  0.0 45.0 jit_solution(4645275809222093589)
XLA Ops:
  0.0 0.0 copy-start
  0.0 0.0 copy-start.1
  0.0 0.0 copy-start.2
  0.0 0.8 %copy.6 = s32[16,64]{0,1:T(8,128)S(1)} copy(s32[16,64]{1,0:T(8,128)} %bitcast.69) | data formatting | bytes 8192 | tf_op jit(solution)/shard_map/eq | solution.py:16
  0.8 0.0 copy-done
  0.8 0.4 convolution_convert_fusion
  1.2 0.8 %copy.7 = bf16[16,64,128]{2,1,0:T(8,128)(2,1)} copy(bf16[16,64,128]{2,0,1:T(8,128)(2,1)S(1)} %convolution_convert_fusion) | data formatting | bytes 524288 | tf_op jit(solution)/shard_map/convert_element_type | solution.py:17
  2.0 7.6 %all-to-all-start = ((bf16[16,64,128]{2,1,0:T(8,128)(2,1)}), bf16[16,64,128]{2,1,0:T(8,128)(2,1)S(1)}, u32[]{:S(2)}, u32[]{:S(2)}) async-start(bf16[16,64,128]{2,1,0:T(8,128)(2,1)} %copy.7), calls=%async_computation | async-start | bytes 524288 | tf_op jit(solution)/shard_map/all_to_all | solution.py:18
  9.5 0.0 copy-done.1
  9.6 0.0 copy-done.2
  9.6 7.4 %all-to-all-done = bf16[16,64,128]{2,1,0:T(8,128)(2,1)S(1)} async-done(((bf16[16,64,128]{2,1,0:T(8,128)(2,1)}), bf16[16,64,128]{2,1,0:T(8,128)(2,1)S(1)}, u32[]{:S(2)}, u32[]{:S(2)}) %all-to-all-start) | async-done | bytes 262176 | tf_op jit(solution)/shard_map/all_to_all | solution.py:18
  17.0 0.2 copy.8
  17.2 0.7 %gather_fusion = bf16[160,16,128]{2,1,0:T(8,128)(2,1)S(1)} fusion(bf16[16,64,128]{2,0,1:T(8,128)(2,1)S(1)} %copy.8, s32[1024]{0:T(1024)S(1)} %pad_clamp_fusion), kind=kCustom, calls=%fused_computation | custom fusion | bytes 1311360 | tf_op jit(solution)/shard_map/jit(_take)/gather | solution.py:46
  17.9 3.5 %fusion = f32[160,16,128]{2,1,0:T(8,128)S(1)} fusion(bf16[1,1,160,128,128]{4,3,2,1,0:T(8,128)(2,1)} %param.6, bf16[160,16,128]{2,1,0:T(8,128)(2,1)S(1)} %gather_fusion, pred[160]{0:T(512)(128)(4,1)S(1)} %compare_and_fusion), kind=kOutput, calls=%fused_computation.1 | convolution fusion | flops 84213760 | bytes 7209120 | tf_op jit(solution)/shard_map/pst,stu->spu/dot_general | solution.py:47
  21.4 0.5 %copy.14 = bf16[20,8,16,128]{3,1,2,0:T(8,128)(2,1)S(1)} copy(f32[20,8,16,128]{3,2,1,0:T(8,128)S(1)} %bitcast.63) | data formatting | bytes 1966080
  21.9 0.2 fusion.11
  22.2 0.6 %fusion.3 = f32[8,8,16,128]{3,1,2,0:T(8,128)S(1)} fusion(f32[64,2048]{1,0:T(8,128)S(1)} %fusion.11, bf16[160,2048]{1,0:T(8,128)(2,1)S(1)} %bitcast.66, f32[20,8,16,128]{3,2,1,0:T(8,128)S(1)} %bitcast.64, s32[160]{0:T(256)S(1)} %fusion.23), kind=kOutput, calls=%fused_computation.7 | convolution fusion | flops 43067392 | bytes 3015296 | tf_op jit(solution)/shard_map/dot_general | solution.py:55
  22.7 0.1 copy.10
  22.8 2.1 %collective-permute-start = (f32[8,4,16,128]{3,2,1,0:T(8,128)S(1)}, f32[8,4,16,128]{3,2,1,0:T(8,128)S(1)}, u32[]{:S(2)}, u32[]{:S(2)}) collective-permute-start(f32[8,4,16,128]{3,2,1,0:T(8,128)S(1)} %dynamic-slice_bitcast_fusion), channel_id=1, source_target_pairs={{0,1},{1,0},{2,3},{3,2},{4,5},{5,4},{6,7},{7,6},{8,9},{9,8},{10,11... | collective-permute-start | bytes 786440 | tf_op jit(solution)/shard_map/ppermute | solution.py:26
  25.0 1.2 %collective-permute-done = f32[8,4,16,128]{3,2,1,0:T(8,128)S(1)} collective-permute-done((f32[8,4,16,128]{3,2,1,0:T(8,128)S(1)}, f32[8,4,16,128]{3,2,1,0:T(8,128)S(1)}, u32[]{:S(2)}, u32[]{:S(2)}) %collective-permute-start) | collective-permute-done | bytes 262176 | tf_op jit(solution)/shard_map/ppermute | solution.py:26
  26.2 5.7 %collective-permute-start.7 = (f32[4,16,128]{2,1,0:T(8,128)S(1)}, f32[4,16,128]{2,1,0:T(8,128)S(1)}, u32[]{:S(2)}, u32[]{:S(2)}) collective-permute-start(f32[4,16,128]{2,1,0:T(8,128)S(1)} %get-tuple-element.6), channel_id=1, source_target_pairs={{0,14},{2,0},{4,2},{6,4},{8,6},{10,8},{12,10},{14,12},{1,15},{3,1}... | collective-permute-start | bytes 98312 | tf_op jit(solution)/shard_map/ppermute | solution.py:31
  31.9 1.2 %collective-permute-start.6 = (f32[4,16,128]{2,1,0:T(8,128)S(1)}, f32[4,16,128]{2,1,0:T(8,128)S(1)}, u32[]{:S(2)}, u32[]{:S(2)}) collective-permute-start(f32[4,16,128]{2,1,0:T(8,128)S(1)} %get-tuple-element.7), channel_id=1, source_target_pairs={{0,12},{2,14},{4,0},{6,2},{8,4},{10,6},{12,8},{14,10},{1,13},{3,15... | collective-permute-start | bytes 98312 | tf_op jit(solution)/shard_map/ppermute | solution.py:31
  33.0 0.4 collective-permute-start.5
  33.5 4.5 %collective-permute-start.4 = (f32[4,16,128]{2,1,0:T(8,128)S(1)}, f32[4,16,128]{2,1,0:T(8,128)S(1)}, u32[]{:S(2)}, u32[]{:S(2)}) collective-permute-start(f32[4,16,128]{2,1,0:T(8,128)S(1)} %get-tuple-element.9), channel_id=1, source_target_pairs={{0,8},{2,10},{4,12},{6,14},{8,0},{10,2},{12,4},{14,6},{1,9},{3,11}... | collective-permute-start | bytes 98312 | tf_op jit(solution)/shard_map/ppermute | solution.py:31
  38.0 0.0 collective-permute-start.3
  38.0 0.0 collective-permute-done.7
  38.0 2.2 %collective-permute-start.2 = (f32[4,16,128]{2,1,0:T(8,128)S(1)}, f32[4,16,128]{2,1,0:T(8,128)S(1)}, u32[]{:S(2)}, u32[]{:S(2)}) collective-permute-start(f32[4,16,128]{2,1,0:T(8,128)S(1)} %get-tuple-element.11), channel_id=1, source_target_pairs={{0,4},{2,6},{4,8},{6,10},{8,12},{10,14},{12,0},{14,2},{1,5},{3,7},... | collective-permute-start | bytes 98312 | tf_op jit(solution)/shard_map/ppermute | solution.py:31
  40.1 0.0 collective-permute-done.6
  40.1 1.4 %collective-permute-start.1 = (f32[4,16,128]{2,1,0:T(8,128)S(1)}, f32[4,16,128]{2,1,0:T(8,128)S(1)}, u32[]{:S(2)}, u32[]{:S(2)}) collective-permute-start(f32[4,16,128]{2,1,0:T(8,128)S(1)} %get-tuple-element.5), channel_id=1, source_target_pairs={{0,2},{2,4},{4,6},{6,8},{8,10},{10,12},{12,14},{14,0},{1,3},{3,5},... | collective-permute-start | bytes 98312 | tf_op jit(solution)/shard_map/ppermute | solution.py:31
  41.5 0.0 collective-permute-done.5
  41.5 0.0 collective-permute-done.4
  41.5 2.2 %collective-permute-done.3 = f32[4,16,128]{2,1,0:T(8,128)S(1)} collective-permute-done((f32[4,16,128]{2,1,0:T(8,128)S(1)}, f32[4,16,128]{2,1,0:T(8,128)S(1)}, u32[]{:S(2)}, u32[]{:S(2)}) %collective-permute-start.3) | collective-permute-done | bytes 32800 | tf_op jit(solution)/shard_map/ppermute | solution.py:31
  43.7 0.6 %collective-permute-done.2 = f32[4,16,128]{2,1,0:T(8,128)S(1)} collective-permute-done((f32[4,16,128]{2,1,0:T(8,128)S(1)}, f32[4,16,128]{2,1,0:T(8,128)S(1)}, u32[]{:S(2)}, u32[]{:S(2)}) %collective-permute-start.2) | collective-permute-done | bytes 32800 | tf_op jit(solution)/shard_map/ppermute | solution.py:31
  44.4 0.0 collective-permute-done.1
  44.4 0.6 %fusion.18 = bf16[4,16,128]{2,1,0:T(8,128)(2,1)} fusion(f32[4,16,128]{2,1,0:T(8,128)S(1)} %collective-permute-done.7, f32[4,16,128]{2,1,0:T(8,128)S(1)} %collective-permute-done.6, f32[4,16,128]{2,1,0:T(8,128)S(1)} %collective-permute-done.5, f32[4,16,128]{2,1,0:T(8,128)S(1)} %collective-permute-done.4, f32[4,16,128]{2,1,0:T(8,128)S(1)} %collective-permute-done.3, ...), kind=kLoop, calls=%fused_computation.27 | loop fusion | flops 65536 | bytes 278532 | tf_op jit(solution)/shard_map/convert_element_type | solution.py:33
  (7 shorter events, 0.1 us)
Async XLA Ops:
  0.0 0.8 %copy-start = (bf16[1,256,128]{2,1,0:T(8,128)(2,1)S(1)}, bf16[1,256,128]{2,1,0:T(8,128)(2,1)}, u32[]{:S(2)}) copy-start(bf16[1,256,128]{2,1,0:T(8,128)(2,1)} %param.5) | copy-start | bytes 196612
  0.0 9.5 %copy-start.1 = (s32[1,1,160]{2,1,0:T(1,128)S(1)}, s32[1,1,160]{2,1,0:T(1,128)}, u32[]{:S(2)}) copy-start(s32[1,1,160]{2,1,0:T(1,128)} %param.8) | copy-start | bytes 1924
  0.0 9.6 %copy-start.2 = (s32[1,1,160]{2,1,0:T(1,128)S(1)}, s32[1,1,160]{2,1,0:T(1,128)}, u32[]{:S(2)}) copy-start(s32[1,1,160]{2,1,0:T(1,128)} %param.9) | copy-start | bytes 1924
  2.0 15.0 %all-to-all-start = ((bf16[16,64,128]{2,1,0:T(8,128)(2,1)}), bf16[16,64,128]{2,1,0:T(8,128)(2,1)S(1)}, u32[]{:S(2)}, u32[]{:S(2)}) async-start(bf16[16,64,128]{2,1,0:T(8,128)(2,1)} %copy.7), calls=%async_computation | async-start | bytes 524288 | tf_op jit(solution)/shard_map/all_to_all | solution.py:18
  22.8 3.3 %collective-permute-start = (f32[8,4,16,128]{3,2,1,0:T(8,128)S(1)}, f32[8,4,16,128]{3,2,1,0:T(8,128)S(1)}, u32[]{:S(2)}, u32[]{:S(2)}) collective-permute-start(f32[8,4,16,128]{3,2,1,0:T(8,128)S(1)} %dynamic-slice_bitcast_fusion), channel_id=1, source_target_pairs={{0,1},{1,0},{2,3},{3,2},{4,5},{5,4},{6,7},{7,6},{8,9},{9,8},{10,11... | collective-permute-start | bytes 786440 | tf_op jit(solution)/shard_map/ppermute | solution.py:26
  26.2 11.8 %collective-permute-start.7 = (f32[4,16,128]{2,1,0:T(8,128)S(1)}, f32[4,16,128]{2,1,0:T(8,128)S(1)}, u32[]{:S(2)}, u32[]{:S(2)}) collective-permute-start(f32[4,16,128]{2,1,0:T(8,128)S(1)} %get-tuple-element.6), channel_id=1, source_target_pairs={{0,14},{2,0},{4,2},{6,4},{8,6},{10,8},{12,10},{14,12},{1,15},{3,1}... | collective-permute-start | bytes 98312 | tf_op jit(solution)/shard_map/ppermute | solution.py:31
  31.9 8.3 %collective-permute-start.6 = (f32[4,16,128]{2,1,0:T(8,128)S(1)}, f32[4,16,128]{2,1,0:T(8,128)S(1)}, u32[]{:S(2)}, u32[]{:S(2)}) collective-permute-start(f32[4,16,128]{2,1,0:T(8,128)S(1)} %get-tuple-element.7), channel_id=1, source_target_pairs={{0,12},{2,14},{4,0},{6,2},{8,4},{10,6},{12,8},{14,10},{1,13},{3,15... | collective-permute-start | bytes 98312 | tf_op jit(solution)/shard_map/ppermute | solution.py:31
  33.0 8.5 %collective-permute-start.5 = (f32[4,16,128]{2,1,0:T(8,128)S(1)}, f32[4,16,128]{2,1,0:T(8,128)S(1)}, u32[]{:S(2)}, u32[]{:S(2)}) collective-permute-start(f32[4,16,128]{2,1,0:T(8,128)S(1)} %get-tuple-element.8), channel_id=1, source_target_pairs={{0,10},{2,12},{4,14},{6,0},{8,2},{10,4},{12,6},{14,8},{1,11},{3,13... | collective-permute-start | bytes 98312 | tf_op jit(solution)/shard_map/ppermute | solution.py:31
  33.5 8.0 %collective-permute-start.4 = (f32[4,16,128]{2,1,0:T(8,128)S(1)}, f32[4,16,128]{2,1,0:T(8,128)S(1)}, u32[]{:S(2)}, u32[]{:S(2)}) collective-permute-start(f32[4,16,128]{2,1,0:T(8,128)S(1)} %get-tuple-element.9), channel_id=1, source_target_pairs={{0,8},{2,10},{4,12},{6,14},{8,0},{10,2},{12,4},{14,6},{1,9},{3,11}... | collective-permute-start | bytes 98312 | tf_op jit(solution)/shard_map/ppermute | solution.py:31
  38.0 5.8 %collective-permute-start.3 = (f32[4,16,128]{2,1,0:T(8,128)S(1)}, f32[4,16,128]{2,1,0:T(8,128)S(1)}, u32[]{:S(2)}, u32[]{:S(2)}) collective-permute-start(f32[4,16,128]{2,1,0:T(8,128)S(1)} %get-tuple-element.10), channel_id=1, source_target_pairs={{0,6},{2,8},{4,10},{6,12},{8,14},{10,0},{12,2},{14,4},{1,7},{3,9},... | collective-permute-start | bytes 98312 | tf_op jit(solution)/shard_map/ppermute | solution.py:31
  38.0 6.4 %collective-permute-start.2 = (f32[4,16,128]{2,1,0:T(8,128)S(1)}, f32[4,16,128]{2,1,0:T(8,128)S(1)}, u32[]{:S(2)}, u32[]{:S(2)}) collective-permute-start(f32[4,16,128]{2,1,0:T(8,128)S(1)} %get-tuple-element.11), channel_id=1, source_target_pairs={{0,4},{2,6},{4,8},{6,10},{8,12},{10,14},{12,0},{14,2},{1,5},{3,7},... | collective-permute-start | bytes 98312 | tf_op jit(solution)/shard_map/ppermute | solution.py:31
  40.1 4.3 %collective-permute-start.1 = (f32[4,16,128]{2,1,0:T(8,128)S(1)}, f32[4,16,128]{2,1,0:T(8,128)S(1)}, u32[]{:S(2)}, u32[]{:S(2)}) collective-permute-start(f32[4,16,128]{2,1,0:T(8,128)S(1)} %get-tuple-element.5), channel_id=1, source_target_pairs={{0,2},{2,4},{4,6},{6,8},{8,10},{10,12},{12,14},{14,0},{1,3},{3,5},... | collective-permute-start | bytes 98312 | tf_op jit(solution)/shard_map/ppermute | solution.py:31

commit v6 on v5

--- a/solution.py
+++ b/solution.py
@@ -50,10 +50,25 @@
     placed = (owner % nc) * (nz * share) + (owner // nc) * share + slot_ab % share
     upper_part = lax.optimization_barrier(products.astype(jnp.bfloat16))
     lower_part = (products - upper_part.astype(jnp.float32)).astype(jnp.bfloat16)
-    onehot = (placed[None, :] == lax.iota(jnp.int32, AB_DEV)[:, None]).astype(jnp.bfloat16)
-    summed = jnp.dot(onehot, upper_part, preferred_element_type=jnp.float32)
-    summed = summed + jnp.dot(onehot, lower_part, preferred_element_type=jnp.float32)
-    return reduce_rows(summed, nz, nc, share, pairs_all, tile_edge)
+    me_c = lax.axis_index("c")
+    half = nz * share
+    rows_other = (1 - me_c) * half + lax.iota(jnp.int32, half)
+    rows_own = me_c * half + lax.iota(jnp.int32, half)
+
+    def scatter(rows):
+        onehot = (placed[None, :] == rows[:, None]).astype(jnp.bfloat16)
+        total = jnp.dot(onehot, upper_part, preferred_element_type=jnp.float32)
+        return total + jnp.dot(onehot, lower_part, preferred_element_type=jnp.float32)
+
+    other = scatter(rows_other).reshape(nz, share, pairs_all, tile_edge)
+    moved = lax.ppermute(other, "c", [(0, 1), (1, 0)])
+    s = scatter(rows_own).reshape(nz, share, pairs_all, tile_edge) + moved
+    mz = lax.axis_index("z")
+    total = lax.dynamic_index_in_dim(s, mz, 0, keepdims=False)
+    for j in range(1, nz):
+        part = lax.dynamic_index_in_dim(s, (mz + j) % nz, 0, keepdims=False)
+        total = total + lax.ppermute(part, "z", [(i, (i + j) % nz) for i in range(nz)])
+    return total.astype(jnp.bfloat16)
 
 
 def solution(mesh):

time: 45.6 us -> 45.5 us (level)
  waiting for transfers between devices: 11.4 us -> 10.4 us
  matrix products: 4.62 us -> 5.44 us
    ppermute x8, waiting for transfers between devices: 4.06 us -> 3.18 us  [the longest x7 2.89 us: on_device(): lax.ppermute(part, 'z', [(i, (i + j) % nz) for i in range(nz)])]
    dot_general x2 -> x4, matrix products: 0.8 us -> 1.62 us  [the longest x2 1.1 us: scatter(): jnp.dot(onehot, lower_part, preferred_element_type=jnp.float32)]
  transfers between devices with their start and end apart: 9 -> 9, of which waited for: 4 -> 4; matrix products, arithmetic and copies ran while one was open for 0% -> 2% of each run, Pallas kernels for 0% -> 0%
where the time goes in v6:
time: 45.5 us; the launch traced here: 45 us
  starting transfers between devices  25 us (55%)
  waiting for transfers between devices  10.4 us (23%)
  matrix products  5.44 us (12%)
  local copies, waits for them, and re-layouts  3.16 us (7%)
  other arithmetic  0.71 us (2%)
    ppermute x7, starting transfers between devices, on_device(): lax.ppermute(part, 'z', [(i, (i + j) % nz) for i in range(nz)])  15.3 us
    all_to_all x1, starting transfers between devices, gather_rows(): return lax.all_to_all(send, 'row', 0, 0, tiled=True)  7.57 us
    all_to_all x1, waiting for transfers between devices, gather_rows(): return lax.all_to_all(send, 'row', 0, 0, tiled=True)  7.23 us
    dot_general x1, matrix products, on_device(): jnp.einsum('pst,stu->spu', picked, blocks, preferred_element_type=jnp.flo...  3.47 us
    ppermute x7, waiting for transfers between devices, on_device(): lax.ppermute(part, 'z', [(i, (i + j) % nz) for i in range(nz)])  2.89 us
    ppermute x1, starting transfers between devices, on_device(): moved = lax.ppermute(other, 'c', [(0, 1), (1, 0)])  2.11 us
    dot_general x2, matrix products, scatter(): jnp.dot(onehot, lower_part, preferred_element_type=jnp.float32)  1.1 us
  transfers between devices with their start and end apart: 9, of which 4 were waited for; matrix products, arithmetic and copies ran while one was open for 2% of the time, Pallas kernels for 0%

profile of v6, /device:TPU:1, one launch (start us, length us, event | category | flops | bytes accessed | tf_op | source)
XLA Modules:
  0.0 45.0 jit_solution(17568662606246780330)
XLA Ops:
  0.0 0.0 copy-start
  0.0 0.0 copy-start.1
  0.0 0.0 copy-start.2
  0.0 0.8 %copy.6 = s32[16,64]{0,1:T(8,128)S(1)} copy(s32[16,64]{1,0:T(8,128)} %bitcast.74) | data formatting | bytes 8192 | tf_op jit(solution)/shard_map/eq | solution.py:16
  0.8 0.0 copy-done
  0.8 0.4 convolution_convert_fusion
  1.2 0.8 %copy.7 = bf16[16,64,128]{2,1,0:T(8,128)(2,1)} copy(bf16[16,64,128]{2,0,1:T(8,128)(2,1)S(1)} %convolution_convert_fusion) | data formatting | bytes 524288 | tf_op jit(solution)/shard_map/convert_element_type | solution.py:17
  2.0 7.6 %all-to-all-start = ((bf16[16,64,128]{2,1,0:T(8,128)(2,1)}), bf16[16,64,128]{2,1,0:T(8,128)(2,1)S(1)}, u32[]{:S(2)}, u32[]{:S(2)}) async-start(bf16[16,64,128]{2,1,0:T(8,128)(2,1)} %copy.7), calls=%async_computation | async-start | bytes 524288 | tf_op jit(solution)/shard_map/all_to_all | solution.py:18
  9.5 0.0 copy-done.1
  9.7 0.0 copy-done.2
  9.8 7.2 %all-to-all-done = bf16[16,64,128]{2,1,0:T(8,128)(2,1)S(1)} async-done(((bf16[16,64,128]{2,1,0:T(8,128)(2,1)}), bf16[16,64,128]{2,1,0:T(8,128)(2,1)S(1)}, u32[]{:S(2)}, u32[]{:S(2)}) %all-to-all-start) | async-done | bytes 262176 | tf_op jit(solution)/shard_map/all_to_all | solution.py:18
  17.0 0.2 copy.8
  17.2 0.7 %gather_fusion = bf16[160,16,128]{2,1,0:T(8,128)(2,1)S(1)} fusion(bf16[16,64,128]{2,0,1:T(8,128)(2,1)S(1)} %copy.8, s32[1024]{0:T(1024)S(1)} %pad_clamp_fusion), kind=kCustom, calls=%fused_computation | custom fusion | bytes 1311360 | tf_op jit(solution)/shard_map/jit(_take)/gather | solution.py:46
  17.9 3.5 %fusion = f32[160,16,128]{2,1,0:T(8,128)S(1)} fusion(bf16[1,1,160,128,128]{4,3,2,1,0:T(8,128)(2,1)} %param.6, bf16[160,16,128]{2,1,0:T(8,128)(2,1)S(1)} %gather_fusion, pred[160]{0:T(512)(128)(4,1)S(1)} %compare_and_fusion), kind=kOutput, calls=%fused_computation.1 | convolution fusion | flops 84213760 | bytes 7209120 | tf_op jit(solution)/shard_map/pst,stu->spu/dot_general | solution.py:47
  21.4 0.5 %copy.16 = bf16[20,8,16,128]{3,1,2,0:T(8,128)(2,1)S(1)} copy(f32[20,8,16,128]{3,2,1,0:T(8,128)S(1)} %bitcast.65) | data formatting | bytes 1966080
  21.9 0.3 fusion.12
  22.2 0.6 %fusion.4 = f32[4,8,16,128]{3,1,2,0:T(8,128)S(1)} fusion(f32[32,2048]{1,0:T(8,128)S(1)} %fusion.12, s32[160]{0:T(256)S(1)} %fusion.34, s32[32]{0:T(128)S(1)} %iota_add_fusion, bf16[160,2048]{1,0:T(8,128)(2,1)S(1)} %bitcast.69, f32[20,8,16,128]{3,2,1,0:T(8,128)S(1)} %bitcast.66), kind=kOutput, calls=%fused_computation.10 | convolution fusion | flops 22025216 | bytes 2491136 | tf_op jit(solution)/shard_map/dot_general | solution.py:61
  22.8 2.1 %collective-permute-start = (f32[8,4,16,128]{3,2,1,0:T(8,128)S(1)}, f32[8,4,16,128]{3,2,1,0:T(8,128)S(1)}, u32[]{:S(2)}, u32[]{:S(2)}) collective-permute-start(f32[8,4,16,128]{3,2,1,0:T(8,128)S(1)} %bitcast.73), channel_id=1, source_target_pairs={{0,1},{1,0},{2,3},{3,2},{4,5},{5,4},{6,7},{7,6},{8,9},{9,8},{10,11... | collective-permute-start | bytes 786440 | tf_op jit(solution)/shard_map/ppermute | solution.py:64
  24.9 0.3 fusion.15
  25.2 0.6 %fusion.3 = f32[4,8,16,128]{3,1,2,0:T(8,128)S(1)} fusion(f32[32,2048]{1,0:T(8,128)S(1)} %fusion.15, s32[160]{0:T(256)S(1)} %fusion.34, s32[32]{0:T(128)S(1)} %iota_add_fusion.1, bf16[160,2048]{1,0:T(8,128)(2,1)S(1)} %bitcast.71, f32[20,8,16,128]{3,2,1,0:T(8,128)S(1)} %bitcast.67), kind=kOutput, calls=%fused_computation.9 | convolution fusion | flops 22025216 | bytes 2491136 | tf_op jit(solution)/shard_map/dot_general | solution.py:61
  25.8 0.3 collective-permute-done
  26.1 5.7 %collective-permute-start.7 = (f32[4,16,128]{2,1,0:T(8,128)S(1)}, f32[4,16,128]{2,1,0:T(8,128)S(1)}, u32[]{:S(2)}, u32[]{:S(2)}) collective-permute-start(f32[4,16,128]{2,1,0:T(8,128)S(1)} %get-tuple-element.6), channel_id=1, source_target_pairs={{0,14},{2,0},{4,2},{6,4},{8,6},{10,8},{12,10},{14,12},{1,15},{3,1}... | collective-permute-start | bytes 98312 | tf_op jit(solution)/shard_map/ppermute | solution.py:70
  31.8 1.2 %collective-permute-start.6 = (f32[4,16,128]{2,1,0:T(8,128)S(1)}, f32[4,16,128]{2,1,0:T(8,128)S(1)}, u32[]{:S(2)}, u32[]{:S(2)}) collective-permute-start(f32[4,16,128]{2,1,0:T(8,128)S(1)} %get-tuple-element.7), channel_id=1, source_target_pairs={{0,12},{2,14},{4,0},{6,2},{8,4},{10,6},{12,8},{14,10},{1,13},{3,15... | collective-permute-start | bytes 98312 | tf_op jit(solution)/shard_map/ppermute | solution.py:70
  33.0 0.4 collective-permute-start.5
  33.4 4.5 %collective-permute-start.4 = (f32[4,16,128]{2,1,0:T(8,128)S(1)}, f32[4,16,128]{2,1,0:T(8,128)S(1)}, u32[]{:S(2)}, u32[]{:S(2)}) collective-permute-start(f32[4,16,128]{2,1,0:T(8,128)S(1)} %get-tuple-element.9), channel_id=1, source_target_pairs={{0,8},{2,10},{4,12},{6,14},{8,0},{10,2},{12,4},{14,6},{1,9},{3,11}... | collective-permute-start | bytes 98312 | tf_op jit(solution)/shard_map/ppermute | solution.py:70
  37.9 0.0 collective-permute-start.3
  37.9 0.0 collective-permute-done.7
  37.9 2.2 %collective-permute-start.2 = (f32[4,16,128]{2,1,0:T(8,128)S(1)}, f32[4,16,128]{2,1,0:T(8,128)S(1)}, u32[]{:S(2)}, u32[]{:S(2)}) collective-permute-start(f32[4,16,128]{2,1,0:T(8,128)S(1)} %get-tuple-element.11), channel_id=1, source_target_pairs={{0,4},{2,6},{4,8},{6,10},{8,12},{10,14},{12,0},{14,2},{1,5},{3,7},... | collective-permute-start | bytes 98312 | tf_op jit(solution)/shard_map/ppermute | solution.py:70
  40.1 0.0 collective-permute-done.6
  40.1 1.4 %collective-permute-start.1 = (f32[4,16,128]{2,1,0:T(8,128)S(1)}, f32[4,16,128]{2,1,0:T(8,128)S(1)}, u32[]{:S(2)}, u32[]{:S(2)}) collective-permute-start(f32[4,16,128]{2,1,0:T(8,128)S(1)} %get-tuple-element.5), channel_id=1, source_target_pairs={{0,2},{2,4},{4,6},{6,8},{8,10},{10,12},{12,14},{14,0},{1,3},{3,5},... | collective-permute-start | bytes 98312 | tf_op jit(solution)/shard_map/ppermute | solution.py:70
  41.4 0.0 collective-permute-done.5
  41.4 0.0 collective-permute-done.4
  41.4 2.2 %collective-permute-done.3 = f32[4,16,128]{2,1,0:T(8,128)S(1)} collective-permute-done((f32[4,16,128]{2,1,0:T(8,128)S(1)}, f32[4,16,128]{2,1,0:T(8,128)S(1)}, u32[]{:S(2)}, u32[]{:S(2)}) %collective-permute-start.3) | collective-permute-done | bytes 32800 | tf_op jit(solution)/shard_map/ppermute | solution.py:70
  43.7 0.6 %collective-permute-done.2 = f32[4,16,128]{2,1,0:T(8,128)S(1)} collective-permute-done((f32[4,16,128]{2,1,0:T(8,128)S(1)}, f32[4,16,128]{2,1,0:T(8,128)S(1)}, u32[]{:S(2)}, u32[]{:S(2)}) %collective-permute-start.2) | collective-permute-done | bytes 32800 | tf_op jit(solution)/shard_map/ppermute | solution.py:70
  44.3 0.0 collective-permute-done.1
  44.3 0.6 %fusion.23 = bf16[4,16,128]{2,1,0:T(8,128)(2,1)} fusion(f32[4,16,128]{2,1,0:T(8,128)S(1)} %collective-permute-done.7, f32[4,16,128]{2,1,0:T(8,128)S(1)} %collective-permute-done.6, f32[4,16,128]{2,1,0:T(8,128)S(1)} %collective-permute-done.5, f32[4,16,128]{2,1,0:T(8,128)S(1)} %collective-permute-done.4, f32[4,16,128]{2,1,0:T(8,128)S(1)} %collective-permute-done.3, ...), kind=kLoop, calls=%fused_computation.31 | loop fusion | flops 65536 | bytes 278532 | tf_op jit(solution)/shard_map/convert_element_type | solution.py:71
  (10 shorter events, 0.2 us)
Async XLA Ops:
  0.0 0.8 %copy-start = (bf16[1,256,128]{2,1,0:T(8,128)(2,1)S(1)}, bf16[1,256,128]{2,1,0:T(8,128)(2,1)}, u32[]{:S(2)}) copy-start(bf16[1,256,128]{2,1,0:T(8,128)(2,1)} %param.5) | copy-start | bytes 196612
  0.0 9.5 %copy-start.1 = (s32[1,1,160]{2,1,0:T(1,128)S(1)}, s32[1,1,160]{2,1,0:T(1,128)}, u32[]{:S(2)}) copy-start(s32[1,1,160]{2,1,0:T(1,128)} %param.8) | copy-start | bytes 1924
  0.0 9.7 %copy-start.2 = (s32[1,1,160]{2,1,0:T(1,128)S(1)}, s32[1,1,160]{2,1,0:T(1,128)}, u32[]{:S(2)}) copy-start(s32[1,1,160]{2,1,0:T(1,128)} %param.9) | copy-start | bytes 1924
  2.0 15.0 %all-to-all-start = ((bf16[16,64,128]{2,1,0:T(8,128)(2,1)}), bf16[16,64,128]{2,1,0:T(8,128)(2,1)S(1)}, u32[]{:S(2)}, u32[]{:S(2)}) async-start(bf16[16,64,128]{2,1,0:T(8,128)(2,1)} %copy.7), calls=%async_computation | async-start | bytes 524288 | tf_op jit(solution)/shard_map/all_to_all | solution.py:18
  22.8 3.3 %collective-permute-start = (f32[8,4,16,128]{3,2,1,0:T(8,128)S(1)}, f32[8,4,16,128]{3,2,1,0:T(8,128)S(1)}, u32[]{:S(2)}, u32[]{:S(2)}) collective-permute-start(f32[8,4,16,128]{3,2,1,0:T(8,128)S(1)} %bitcast.73), channel_id=1, source_target_pairs={{0,1},{1,0},{2,3},{3,2},{4,5},{5,4},{6,7},{7,6},{8,9},{9,8},{10,11... | collective-permute-start | bytes 786440 | tf_op jit(solution)/shard_map/ppermute | solution.py:64
  26.1 11.8 %collective-permute-start.7 = (f32[4,16,128]{2,1,0:T(8,128)S(1)}, f32[4,16,128]{2,1,0:T(8,128)S(1)}, u32[]{:S(2)}, u32[]{:S(2)}) collective-permute-start(f32[4,16,128]{2,1,0:T(8,128)S(1)} %get-tuple-element.6), channel_id=1, source_target_pairs={{0,14},{2,0},{4,2},{6,4},{8,6},{10,8},{12,10},{14,12},{1,15},{3,1}... | collective-permute-start | bytes 98312 | tf_op jit(solution)/shard_map/ppermute | solution.py:70
  31.8 8.3 %collective-permute-start.6 = (f32[4,16,128]{2,1,0:T(8,128)S(1)}, f32[4,16,128]{2,1,0:T(8,128)S(1)}, u32[]{:S(2)}, u32[]{:S(2)}) collective-permute-start(f32[4,16,128]{2,1,0:T(8,128)S(1)} %get-tuple-element.7), channel_id=1, source_target_pairs={{0,12},{2,14},{4,0},{6,2},{8,4},{10,6},{12,8},{14,10},{1,13},{3,15... | collective-permute-start | bytes 98312 | tf_op jit(solution)/shard_map/ppermute | solution.py:70
  33.0 8.5 %collective-permute-start.5 = (f32[4,16,128]{2,1,0:T(8,128)S(1)}, f32[4,16,128]{2,1,0:T(8,128)S(1)}, u32[]{:S(2)}, u32[]{:S(2)}) collective-permute-start(f32[4,16,128]{2,1,0:T(8,128)S(1)} %get-tuple-element.8), channel_id=1, source_target_pairs={{0,10},{2,12},{4,14},{6,0},{8,2},{10,4},{12,6},{14,8},{1,11},{3,13... | collective-permute-start | bytes 98312 | tf_op jit(solution)/shard_map/ppermute | solution.py:70
  33.4 8.0 %collective-permute-start.4 = (f32[4,16,128]{2,1,0:T(8,128)S(1)}, f32[4,16,128]{2,1,0:T(8,128)S(1)}, u32[]{:S(2)}, u32[]{:S(2)}) collective-permute-start(f32[4,16,128]{2,1,0:T(8,128)S(1)} %get-tuple-element.9), channel_id=1, source_target_pairs={{0,8},{2,10},{4,12},{6,14},{8,0},{10,2},{12,4},{14,6},{1,9},{3,11}... | collective-permute-start | bytes 98312 | tf_op jit(solution)/shard_map/ppermute | solution.py:70
  37.9 5.8 %collective-permute-start.3 = (f32[4,16,128]{2,1,0:T(8,128)S(1)}, f32[4,16,128]{2,1,0:T(8,128)S(1)}, u32[]{:S(2)}, u32[]{:S(2)}) collective-permute-start(f32[4,16,128]{2,1,0:T(8,128)S(1)} %get-tuple-element.10), channel_id=1, source_target_pairs={{0,6},{2,8},{4,10},{6,12},{8,14},{10,0},{12,2},{14,4},{1,7},{3,9},... | collective-permute-start | bytes 98312 | tf_op jit(solution)/shard_map/ppermute | solution.py:70
  37.9 6.4 %collective-permute-start.2 = (f32[4,16,128]{2,1,0:T(8,128)S(1)}, f32[4,16,128]{2,1,0:T(8,128)S(1)}, u32[]{:S(2)}, u32[]{:S(2)}) collective-permute-start(f32[4,16,128]{2,1,0:T(8,128)S(1)} %get-tuple-element.11), channel_id=1, source_target_pairs={{0,4},{2,6},{4,8},{6,10},{8,12},{10,14},{12,0},{14,2},{1,5},{3,7},... | collective-permute-start | bytes 98312 | tf_op jit(solution)/shard_map/ppermute | solution.py:70
  40.1 4.3 %collective-permute-start.1 = (f32[4,16,128]{2,1,0:T(8,128)S(1)}, f32[4,16,128]{2,1,0:T(8,128)S(1)}, u32[]{:S(2)}, u32[]{:S(2)}) collective-permute-start(f32[4,16,128]{2,1,0:T(8,128)S(1)} %get-tuple-element.5), channel_id=1, source_target_pairs={{0,2},{2,4},{4,6},{6,8},{8,10},{10,12},{12,14},{14,0},{1,3},{3,5},... | collective-permute-start | bytes 98312 | tf_op jit(solution)/shard_map/ppermute | solution.py:70
